TPU v7x, 256 devices: a whole 4x4x8 slice. The times are simulated.
256 devices in a mesh: doc: 8 (over y, core), seq: 32 (over z, x).
Axes of the slice: x: 4, y: 4, z: 8, core: 2. Of those that a mesh axis runs over, the one named last changes fastest.
Arguments:
- queries: bfloat16 [163840, 4096], P(('doc', 'seq')), parts along dimension 0, may hold values from -75 to 75
- memory_kv: bfloat16 [256, 384, 1024], P(('doc', 'seq')), parts along dimension 0, may hold values from -8 to 8
- block_image: int32 [1280], P(('doc', 'seq')), parts along dimension 0, may hold values from -1 to 31
- image_slot: int32 [256], P('doc'), parts along dimension 0, may hold values from 0 to 31, each once
Outputs:
- context: bfloat16 [163840, 4096], P(('doc', 'seq')), parts along dimension 0
There are 8 independent parts, one for each index of `doc`. A program takes and returns all parts, laid end to end along the dimension named above; each array names one. Nothing has to cross between parts.
Inputs may be any that keep to these rules, and one draw needn't show every extreme that they name: `block_image`: -1 marks a block without an image. A permutation: image i is held by seq index image_slot[i].
All inputs are finite; a program needn't handle non-finite values.
Results may differ from a plain program's by a relative error of at most 0.0049.
Values may be sent and summed in bfloat16 or wider, within the bound.
No kernel may reach another device: no remote copies, remote signals or barrier semaphores. Data moves between devices by JAX's collectives and lax.ppermute only.
A program may use at most 192 MiB of HBM per device.

v0:
```python
import jax
import jax.numpy as jnp
from jax import lax
from jax.sharding import PartitionSpec as P

HD = 128
KV_HEADS = 4
BLOCK = 128


def holder_of(image_ids, image_slot):
    image_count = image_slot.shape[0]
    same_image = image_ids[:, None] == jnp.arange(image_count, dtype=jnp.int32)[None, :]
    return jnp.sum(jnp.where(same_image, image_slot[None, :], 0), axis=1)


def attend_core(query_blocks, image_ids, block_memory, kv_local):
    count_blocks, block_rows, row_width = query_blocks.shape
    group_size = row_width // (HD * kv_local)
    memory_rows = block_memory.reshape(count_blocks, block_memory.shape[1], kv_local, 2, HD)
    query_heads = query_blocks.reshape(count_blocks, block_rows, kv_local, group_size, HD)
    scores = jnp.einsum(
        "nrhgd,nkhd->nhgrk",
        query_heads,
        memory_rows[:, :, :, 0],
        preferred_element_type=jnp.float32,
    ) * HD ** (-0.5)
    row_max = jnp.max(scores, axis=-1, keepdims=True)
    weights = jnp.exp(scores - row_max)
    attn_weights = (weights / jnp.sum(weights, axis=-1, keepdims=True)).astype(jnp.bfloat16)
    context = jnp.einsum(
        "nhgrk,nkhd->nrhgd",
        attn_weights,
        memory_rows[:, :, :, 1],
        preferred_element_type=jnp.float32,
    )
    has_image = (image_ids >= 0)[:, None, None, None, None]
    context = jnp.where(has_image, context, 0.0)
    return context.reshape(count_blocks, block_rows, row_width).astype(jnp.bfloat16)


def local(queries, memory_kv, block_image, image_slot):
    row_count, row_width = queries.shape
    query_blocks = queries.reshape(row_count // BLOCK, BLOCK, row_width)
    seq_count = lax.axis_size("seq")
    own_blocks = block_image.shape[0]
    wanted = lax.all_gather(block_image, "seq", axis=0, tiled=True)
    column_share = lax.all_to_all(memory_kv, "seq", split_axis=2, concat_axis=0, tiled=True)
    wanted_slot = holder_of(wanted, image_slot)
    outgoing = jnp.take(column_share, wanted_slot, axis=0)
    outgoing = outgoing.reshape(seq_count, own_blocks, column_share.shape[1], column_share.shape[2])
    arrived = lax.all_to_all(outgoing, "seq", split_axis=0, concat_axis=3, tiled=True)
    result = attend_core(query_blocks, block_image, arrived[0], KV_HEADS)
    return result.reshape(row_count, row_width)


def solution(mesh):
    placed = (P(("doc", "seq"), None), P(("doc", "seq"), None, None), P(("doc", "seq")), P("doc"))
    return jax.shard_map(
        local, mesh=mesh, in_specs=placed, out_specs=P(("doc", "seq"), None), check_vma=False
    )
```

profile of v0, /device:TPU:16, one launch (start us, length us, event | category | flops | bytes accessed | tf_op | source)
XLA Modules:
  0.0 239.7 jit_solution(13762202509634023614)
XLA Ops:
  0.0 4.2 %copy.22 = bf16[1,384,1024]{1,0,2:T(2,128)(2,1)S(1)} copy(bf16[1,384,1024]{2,1,0:T(8,128)(2,1)} %param.5) | data formatting | bytes 1572864 | tf_op args[1]
  4.2 0.5 broadcast.50
  4.7 5.4 %reduce = bf16[1024,384]{1,0:T(8,128)(2,1)S(1)} reduce(bf16[1024,1,384]{2,1,0:T(2,128)(2,1)S(1)} %bitcast.53, bf16[]{:T(256)} %broadcast.50), dimensions={1}, to_apply=%bitcast.44.reduce_sub_computation | reduce | bytes 1572866
  10.1 1.1 reshape.47
  11.2 11.3 %all-to-all-start = ((bf16[32,2,6144]{2,1,0:T(2,128)(2,1)}), bf16[32,2,6144]{2,1,0:T(2,128)(2,1)S(1)}, u32[]{:S(2)}, u32[]{:S(2)}) async-start(bf16[32,2,6144]{2,1,0:T(2,128)(2,1)} %reshape.47), calls=%async_computation | async-start | bytes 1572864 | tf_op jit(solution)/shard_map/all_to_all | solution.py:48
  22.5 0.7 dynamic-slice
  23.9 0.2 dynamic-update-slice
  24.2 25.1 %all-reduce = s32[160]{0:T(256)S(1)} all-reduce(s32[160]{0:T(256)S(1)} %dynamic-update-slice), channel_id=1, replica_groups=mesh['doc'=8,'seq'=32] {'seq'}, use_global_device_ids=true, to_apply=%add | all-reduce | flops 160 | bytes 1280
  49.2 0.1 select_reduce_fusion
  49.3 0.1 reduce_sum.23
  49.5 0.0 all-to-all-done
  49.5 0.8 reshape.48
  50.3 0.1 copy.32
  50.4 3.4 %gather_fusion = bf16[160,384,32]{1,2,0:T(8,128)(2,1)} fusion(bf16[32,384,32]{1,2,0:T(8,128)(2,1)S(1)} %bitcast.48, s32[1024]{0:T(1024)S(1)} %pad_clamp_fusion), kind=kCustom, calls=%fused_computation | custom fusion | bytes 7864960 | tf_op jit(solution)/shard_map/jit(_take)/gather | solution.py:50
  53.8 4.5 %broadcast_select_fusion = bf16[32,5,384,32]{2,3,1,0:T(8,128)(2,1)} fusion(bf16[32,5,384,32]{2,3,1,0:T(8,128)(2,1)} %bitcast.49, pred[32,5]{1,0:T(8,128)(4,1)S(1)} %compare_and_fusion), kind=kLoop, calls=%fused_computation.14 | loop fusion | flops 1966080 | bytes 7864480 | tf_op jit(solution)/shard_map/jit(_take)/select_n | solution.py:50
  58.3 8.2 %all-to-all-start.1 = ((bf16[32,5,384,32]{2,3,1,0:T(8,128)(2,1)}), bf16[32,5,384,32]{2,3,1,0:T(8,128)(2,1)}, u32[]{:S(2)}, u32[]{:S(2)}) async-start(bf16[32,5,384,32]{2,3,1,0:T(8,128)(2,1)} %broadcast_select_fusion), calls=%async_computation.1 | async-start | bytes 7864320 | tf_op jit(solution)/shard_map/all_to_all | solution.py:52
  66.5 6.5 %copy.35 = bf16[80,8,32,128]{3,2,1,0:T(8,128)(2,1)} copy(bf16[80,8,32,128]{3,1,2,0:T(8,128)(2,1)} %bitcast.55) | data formatting | bytes 10485760
  73.0 79.6 %all-to-all-done.1 = bf16[32,5,384,32]{2,3,1,0:T(8,128)(2,1)} async-done(((bf16[32,5,384,32]{2,3,1,0:T(8,128)(2,1)}), bf16[32,5,384,32]{2,3,1,0:T(8,128)(2,1)}, u32[]{:S(2)}, u32[]{:S(2)}) %all-to-all-start.1) | async-done | bytes 3932192 | tf_op jit(solution)/shard_map/all_to_all | solution.py:52
  152.6 4.5 %copy.23 = bf16[1,5,384,32,32]{2,4,3,1,0:T(8,128)(2,1)} copy(bf16[1,5,384,32,32]{2,4,1,3,0:T(8,128)(2,1)} %bitcast.7) | data formatting | bytes 7864320 | tf_op jit(solution)/shard_map/all_to_all | solution.py:52
  157.1 17.8 %fusion.9 = f32[5,4,384,128,8]{3,2,4,1,0:T(8,128)} fusion(bf16[5,128,4,8,128]{4,3,2,1,0:T(8,128)(2,1)} %bitcast.50, bf16[5,384,4,2,128]{1,4,3,2,0:T(8,128)(2,1)} %bitcast.51), kind=kOutput, calls=%fused_computation.12 | convolution fusion | flops 2013265920 | bytes 38666240 | tf_op jit(solution)/shard_map/nrhgd,nkhd->nhgrk/dot_general | solution.py:22
  174.9 32.9 %fusion.12 = (f32[5,4,8,128]{3,2,1,0:T(8,128)S(1)}, f32[5,4,8,128,384]{3,4,2,1,0:T(8,128)}) fusion(f32[5,4,384,128,8]{3,2,4,1,0:T(8,128)} %fusion.9), kind=kOutput, calls=%fused_computation.25 | output fusion | flops 31457664 | bytes 62996480 | tf_op jit(solution)/shard_map/sub | solution.py:29
  207.8 14.6 %fusion.8 = bf16[5,128,4,8,128]{1,4,3,2,0:T(8,128)(2,1)} fusion(pred[5]{0:T(512)(128)(4,1)S(1)} %broadcast_compare_fusion, f32[5,4,8,128,384]{3,4,2,1,0:T(8,128)} %get-tuple-element.6, f32[5,4,8,128]{3,2,1,0:T(8,128)S(1)} %get-tuple-element.5, bf16[5,384,4,2,128]{1,4,3,2,0:T(8,128)(2,1)} %bitcast.52), kind=kOutput, calls=%fused_computation.11 | convolution fusion | flops 2034237440 | bytes 38748164 | tf_op jit(solution)/shard_map/nhgrk,nkhd->nrhgd/dot_general | solution.py:31
  222.4 8.5 %copy.28 = bf16[5,128,4,8,128]{4,3,2,1,0:T(8,128)(2,1)} copy(bf16[5,128,4,8,128]{1,4,3,2,0:T(8,128)(2,1)} %fusion.8) | data formatting | bytes 10485760 | tf_op jit(solution)/shard_map/convert_element_type | solution.py:39
  230.9 8.8 %convert_element_type.16 = bf16[640,4096]{1,0:T(8,128)(2,1)} reshape(bf16[5,128,4,8,128]{4,3,2,1,0:T(8,128)(2,1)} %copy.28) | data formatting | bytes 10485760 | tf_op jit(solution)/shard_map/convert_element_type | solution.py:39
  (11 shorter events, 0.0 us)
Async XLA Ops:
  0.0 22.5 %copy-start.2 = (u32[256]{0:T(256)S(1)}, u32[256]{0:T(256)}, u32[]{:S(2)}) copy-start(u32[256]{0:T(256)} %constant.29) | copy-start | bytes 3076
  0.0 23.9 %copy-start.1 = (s32[5]{0:T(128)S(1)}, s32[5]{0:T(128)}, u32[]{:S(2)}) copy-start(s32[5]{0:T(128)} %param.6) | copy-start | bytes 64
  0.0 49.2 %copy-start = (s32[32]{0:T(128)S(1)}, s32[32]{0:T(128)}, u32[]{:S(2)}) copy-start(s32[32]{0:T(128)} %param.7) | copy-start | bytes 388
  11.2 38.3 %all-to-all-start = ((bf16[32,2,6144]{2,1,0:T(2,128)(2,1)}), bf16[32,2,6144]{2,1,0:T(2,128)(2,1)S(1)}, u32[]{:S(2)}, u32[]{:S(2)}) async-start(bf16[32,2,6144]{2,1,0:T(2,128)(2,1)} %reshape.47), calls=%async_computation | async-start | bytes 1572864 | tf_op jit(solution)/shard_map/all_to_all | solution.py:48
  58.3 94.3 %all-to-all-start.1 = ((bf16[32,5,384,32]{2,3,1,0:T(8,128)(2,1)}), bf16[32,5,384,32]{2,3,1,0:T(8,128)(2,1)}, u32[]{:S(2)}, u32[]{:S(2)}) async-start(bf16[32,5,384,32]{2,3,1,0:T(8,128)(2,1)} %broadcast_select_fusion), calls=%async_computation.1 | async-start | bytes 7864320 | tf_op jit(solution)/shard_map/all_to_all | solution.py:52
where the time goes:
time: 241 us; the launch traced here: 240 us
  waiting for transfers between devices  79.6 us (33%)
  other arithmetic  43 us (18%)
  local copies, waits for them, and re-layouts  39.3 us (16%)
  matrix products  32.4 us (13%)
  blocking collectives  25.1 us (10%)
  starting transfers between devices  19.5 us (8%)
    all_to_all x1, waiting for transfers between devices, local(): lax.all_to_all(outgoing, 'seq', split_axis=0, concat_axis=3, tiled=True)  79.6 us
    sub x1, other arithmetic, attend_core(): weights = jnp.exp(scores - row_max)  32.9 us
    unnamed x1, blocking collectives  25.1 us
    dot_general x1, matrix products, attend_core(): jnp.einsum('nrhgd,nkhd->nhgrk', query_heads, memory_rows[:, :, :, 0], pre...  17.8 us
    convert_element_type x2, local copies, waits for them, and re-layouts, attend_core(): context.reshape(count_blocks, block_rows, row_width).astype(jnp.bfloat16)  17.3 us
    dot_general x1, matrix products, attend_core(): jnp.einsum('nhgrk,nkhd->nrhgd', attn_weights, memory_rows[:, :, :, 1], pr...  14.6 us
    unnamed x15, local copies, waits for them, and re-layouts  14.1 us
    all_to_all x1, starting transfers between devices, local(): lax.all_to_all(memory_kv, 'seq', split_axis=2, concat_axis=0, tiled=True)  11.3 us
  transfers between devices with their start and end apart: 2, of which 1 were waited for; matrix products, arithmetic and copies ran while one was open for 3% of the time, Pallas kernels for 0%

commit v1 on v0

v1 whole, which is shorter than its diff:
```python
import functools

import jax
import jax.numpy as jnp
from jax import lax
from jax.experimental import pallas as pl
from jax.experimental.pallas import tpu as pltpu
from jax.sharding import PartitionSpec as P

HD = 128
KV_HEADS = 4
BLOCK = 128
ROW_GROUPS = 8


def attend_kernel(image_ref, q_ref, kv_ref, o_ref, *, group_size, memory_rows):
    b = pl.program_id(0)
    kv = kv_ref[...].reshape(memory_rows, 2 * HD)
    k = kv[:, :HD]
    v = kv[:, HD:]
    valid = image_ref[b] >= 0
    for g in range(group_size):
        q = q_ref[:, g * HD:(g + 1) * HD]
        s = lax.dot_general(q, k, (((1,), (1,)), ((), ())), preferred_element_type=jnp.float32)
        s = s * HD ** (-0.5)
        m = jnp.max(s, axis=-1, keepdims=True)
        w = jnp.exp(s - m)
        inv = 1.0 / jnp.sum(w, axis=-1, keepdims=True)
        p = (w * inv).astype(jnp.bfloat16)
        ctx = jnp.dot(p, v, preferred_element_type=jnp.float32)
        ctx = jnp.where(valid, ctx, 0.0)
        o_ref[:, g * HD:(g + 1) * HD] = ctx.astype(o_ref.dtype)


def attend(queries, kv_shares, block_image):
    row_count, row_width = queries.shape
    _, kv_local, count_blocks, share_rows, _ = kv_shares.shape
    group_size = row_width // (HD * kv_local)
    head_cols = group_size * HD
    kernel = functools.partial(
        attend_kernel, group_size=group_size, memory_rows=ROW_GROUPS * share_rows
    )
    grid_spec = pltpu.PrefetchScalarGridSpec(
        num_scalar_prefetch=1,
        grid=(count_blocks, kv_local),
        in_specs=[
            pl.BlockSpec((BLOCK, head_cols), lambda b, j, img: (b, j)),
            pl.BlockSpec(
                (ROW_GROUPS, None, None, share_rows, 2 * HD),
                lambda b, j, img: (0, j, b, 0, 0),
            ),
        ],
        out_specs=pl.BlockSpec((BLOCK, head_cols), lambda b, j, img: (b, j)),
    )
    return pl.pallas_call(
        kernel,
        grid_spec=grid_spec,
        out_shape=jax.ShapeDtypeStruct(queries.shape, queries.dtype),
    )(block_image, queries, kv_shares)


def local(queries, memory_kv, block_image, image_slot):
    seq_count = lax.axis_size("seq")
    own_blocks = block_image.shape[0]
    _, img_rows, kv_width = memory_kv.shape
    kv_local = kv_width // (2 * HD)
    share_rows = img_rows // ROW_GROUPS
    shares = memory_kv.reshape(ROW_GROUPS, share_rows, kv_local, 2 * HD)
    shares = shares.transpose(0, 2, 1, 3).reshape(seq_count, share_rows, 2 * HD)
    wanted = lax.all_gather(block_image, "seq", axis=0, tiled=True)
    held = lax.all_to_all(shares, "seq", split_axis=0, concat_axis=0, tiled=True)
    wanted_slot = jnp.take(image_slot, jnp.maximum(wanted, 0), axis=0)
    outgoing = jnp.take(held, wanted_slot, axis=0)
    outgoing = outgoing.reshape(seq_count, own_blocks, share_rows, 2 * HD)
    arrived = lax.all_to_all(outgoing, "seq", split_axis=0, concat_axis=0, tiled=True)
    arrived = arrived.reshape(ROW_GROUPS, kv_local, own_blocks, share_rows, 2 * HD)
    return attend(queries, arrived, block_image)


def solution(mesh):
    placed = (P(("doc", "seq"), None), P(("doc", "seq"), None, None), P(("doc", "seq")), P("doc"))
    return jax.shard_map(
        local, mesh=mesh, in_specs=placed, out_specs=P(("doc", "seq"), None), check_vma=False
    )
```

time: 241 us -> 224 us (0.929)
  blocking collectives: 25.1 us -> 121 us
  waiting for transfers between devices: 79.6 us -> 0.01 us
  Pallas kernels: 0 us -> 60 us
  matrix products: 32.4 us -> 0 us
  local copies, waits for them, and re-layouts: 39.3 us -> 8.42 us
  other arithmetic: 43 us -> 22.6 us
  starting transfers between devices: 19.5 us -> 11.3 us
    all_to_all x0 -> x1, blocking collectives: none -> 95.6 us  [local(): lax.all_to_all(outgoing, 'seq', split_axis=0, concat_axis=0, tiled=True)]
    all_to_all x2 -> x1, waiting for transfers between devices: 79.6 us -> 0.01 us  [local(): lax.all_to_all(shares, 'seq', split_axis=0, concat_axis=0, tiled=True)]
    pallas_call x0 -> x1, Pallas kernels: none -> 60 us  [attend(): pl.pallas_call(kernel, grid_spec=grid_spec, out_shape=jax.ShapeDtypeStruc...]
    sub x1 -> x0, other arithmetic: 32.9 us -> none  [attend_core(): weights = jnp.exp(scores - row_max)]
    dot_general x2 -> x0, matrix products: 32.4 us -> none  [the longest x1 17.8 us: attend_core(): jnp.einsum('nrhgd,nkhd->nhgrk', query_heads, memory_rows[:, :, :, 0], pre...]
    and x1, other arithmetic: 0.01 us -> 20 us  [local(): outgoing = jnp.take(held, wanted_slot, axis=0)]
    convert_element_type x2 -> x0, local copies, waits for them, and re-layouts: 17.3 us -> none  [attend_core(): context.reshape(count_blocks, block_rows, row_width).astype(jnp.bfloat16)]
    unnamed x15 -> x9, local copies, waits for them, and re-layouts: 14.1 us -> 0.83 us
  transfers between devices with their start and end apart: 2 -> 1, of which waited for: 1 -> 0; matrix products, arithmetic and copies ran while one was open for 3% -> 10% of each run, Pallas kernels for 0% -> 0%
where the time goes in v1:
time: 224 us
  blocking collectives  121 us (54%)
  Pallas kernels  60 us (27%)
  other arithmetic  22.6 us (10%)
  starting transfers between devices  11.3 us (5%)
  local copies, waits for them, and re-layouts  8.42 us (4%)
    all_to_all x1, blocking collectives, local(): lax.all_to_all(outgoing, 'seq', split_axis=0, concat_axis=0, tiled=True)  95.6 us
    pallas_call x1, Pallas kernels, attend(): pl.pallas_call(kernel, grid_spec=grid_spec, out_shape=jax.ShapeDtypeStruc...  60 us
    unnamed x1, blocking collectives  25.3 us
    and x1, other arithmetic, local(): outgoing = jnp.take(held, wanted_slot, axis=0)  20 us
    all_to_all x1, starting transfers between devices, local(): lax.all_to_all(shares, 'seq', split_axis=0, concat_axis=0, tiled=True)  11.3 us
  transfers between devices with their start and end apart: 1, of which 0 were waited for; matrix products, arithmetic and copies ran while one was open for 10% of the time, Pallas kernels for 0%

profile of v1, /device:TPU:16, one launch (start us, length us, event | category | flops | bytes accessed | tf_op | source)
XLA Modules:
  0.0 223.9 jit_solution(1961508223733316054)
XLA Ops:
  0.0 0.0 copy-start.2
  0.0 0.0 copy-start.1
  0.0 0.0 copy-start
  0.0 2.0 reshape.26
  2.0 1.0 copy.5
  3.0 11.3 %all-to-all-start = ((bf16[32,48,256]{2,1,0:T(8,128)(2,1)}), bf16[32,48,256]{2,1,0:T(8,128)(2,1)S(1)}, u32[]{:S(2)}, u32[]{:S(2)}) async-start(bf16[32,48,256]{2,1,0:T(8,128)(2,1)} %bitcast.34), calls=%async_computation | async-start | bytes 1572864 | tf_op jit(solution)/shard_map/all_to_all | solution.py:71
  14.3 0.0 copy-done.2
  14.3 0.6 dynamic-slice
  15.5 0.0 copy-done.1
  15.5 0.2 dynamic-update-slice
  15.7 25.3 %all-reduce = s32[160]{0:T(256)S(1)} all-reduce(s32[160]{0:T(256)S(1)} %dynamic-update-slice), channel_id=1, replica_groups=mesh['doc'=8,'seq'=32] {'seq'}, use_global_device_ids=true, to_apply=%add | all-reduce | flops 160 | bytes 1280
  41.0 0.0 copy-done
  41.0 0.7 fusion.1
  41.7 0.7 fusion
  42.5 20.0 %compare_and_fusion = (pred[160]{0:T(512)(128)(4,1)S(1)}, s32[160]{0:T(256)S(1)}) fusion(s32[]{:T(128)} %bitcast.32, s32[]{:T(128)} %bitcast.31, s32[]{:T(128)} %bitcast.30, s32[]{:T(128)} %bitcast.29, s32[]{:T(128)} %bitcast.28, s32[]{:T(128)} %bitcast.27, s32[]{:T(128)} %bitcast.26, s32[]{:T(128)} %bitcast.25, s32[]{:T(128)} %bitcast.24, s32[]{:T(128)} %bitcast.23, ...), kind=kLoop, calls=%fused_computation.35 | loop fusion | flops 11360 | bytes 1568 | tf_op jit(solution)/shard_map/jit(_take)/and | solution.py:73
  62.5 0.1 broadcast_in_dim.22
  62.6 0.0 all-to-all-done
  62.6 3.1 %gather_fusion = bf16[160,48,256]{2,1,0:T(8,128)(2,1)} fusion(bf16[32,48,256]{2,1,0:T(8,128)(2,1)S(1)} %all-to-all-done, s32[1024]{0:T(1024)S(1)} %pad_clamp_fusion), kind=kCustom, calls=%fused_computation | custom fusion | bytes 7864960 | tf_op jit(solution)/shard_map/jit(_take)/gather | solution.py:73
  65.7 2.5 %broadcast_select_fusion = bf16[32,5,48,256]{3,2,1,0:T(8,128)(2,1)S(1)} fusion(bf16[32,5,48,256]{3,2,1,0:T(8,128)(2,1)} %bitcast.37, pred[32,5]{1,0:T(8,128)(4,1)S(1)} %broadcast_in_dim.22), kind=kLoop, calls=%fused_computation.1 | loop fusion | flops 1966080 | bytes 7864480 | tf_op jit(solution)/shard_map/jit(_take)/select_n | solution.py:73
  68.2 95.6 %all_to_all.10 = bf16[32,5,48,256]{3,2,1,0:T(8,128)(2,1)} all-to-all(bf16[32,5,48,256]{3,2,1,0:T(8,128)(2,1)S(1)} %broadcast_select_fusion), channel_id=1, replica_groups=mesh['doc'=8,'seq'=32] {'seq'}, dimensions={0} | all-to-all | bytes 7864320 | tf_op jit(solution)/shard_map/all_to_all | solution.py:75
  163.9 60.0 %shard_map.46 = bf16[640,4096]{1,0:T(8,128)(2,1)} custom-call(s32[5]{0:T(128)} %image_ref.1, bf16[640,4096]{1,0:T(8,128)(2,1)} %q_ref.1, bf16[8,4,5,48,256]{4,3,2,1,0:T(8,128)(2,1)} %bitcast.38), custom_call_target="tpu_custom_call" | custom-call | tf_op jit(solution)/shard_map/pallas_call | solution.py:55
  (2 shorter events, 0.0 us)
Async XLA Ops:
  0.0 14.3 %copy-start.2 = (u32[256]{0:T(256)S(1)}, u32[256]{0:T(256)}, u32[]{:S(2)}) copy-start(u32[256]{0:T(256)} %constant.70) | copy-start | bytes 3076
  0.0 15.5 %copy-start.1 = (s32[5]{0:T(128)S(1)}, s32[5]{0:T(128)}, u32[]{:S(2)}) copy-start(s32[5]{0:T(128)} %image_ref.1) | copy-start | bytes 64
  0.0 41.0 %copy-start = (s32[32]{0:T(128)S(1)}, s32[32]{0:T(128)}, u32[]{:S(2)}) copy-start(s32[32]{0:T(128)} %param.7) | copy-start | bytes 388
  3.0 59.6 %all-to-all-start = ((bf16[32,48,256]{2,1,0:T(8,128)(2,1)}), bf16[32,48,256]{2,1,0:T(8,128)(2,1)S(1)}, u32[]{:S(2)}, u32[]{:S(2)}) async-start(bf16[32,48,256]{2,1,0:T(8,128)(2,1)} %bitcast.34), calls=%async_computation | async-start | bytes 1572864 | tf_op jit(solution)/shard_map/all_to_all | solution.py:71

commit v2 on v1

--- a/solution.py
+++ b/solution.py
@@ -11,6 +11,7 @@
 KV_HEADS = 4
 BLOCK = 128
 ROW_GROUPS = 8
+TAG_ROWS = 16
 
 
 def attend_kernel(image_ref, q_ref, kv_ref, o_ref, *, group_size, memory_rows):
@@ -19,17 +20,17 @@
     k = kv[:, :HD]
     v = kv[:, HD:]
     valid = image_ref[b] >= 0
+    q = jnp.concatenate([q_ref[:, g * HD:(g + 1) * HD] for g in range(group_size)], axis=0)
+    s = lax.dot_general(k, q, (((1,), (1,)), ((), ())), preferred_element_type=jnp.float32)
+    s = s * HD ** (-0.5)
+    m = jnp.max(s, axis=0, keepdims=True)
+    w = jnp.exp(s - m)
+    inv = 1.0 / jnp.sum(w, axis=0, keepdims=True)
+    p = (w * inv).astype(jnp.bfloat16)
+    ctx = lax.dot_general(p, v, (((0,), (0,)), ((), ())), preferred_element_type=jnp.float32)
+    ctx = jnp.where(valid, ctx, 0.0).astype(o_ref.dtype)
     for g in range(group_size):
-        q = q_ref[:, g * HD:(g + 1) * HD]
-        s = lax.dot_general(q, k, (((1,), (1,)), ((), ())), preferred_element_type=jnp.float32)
-        s = s * HD ** (-0.5)
-        m = jnp.max(s, axis=-1, keepdims=True)
-        w = jnp.exp(s - m)
-        inv = 1.0 / jnp.sum(w, axis=-1, keepdims=True)
-        p = (w * inv).astype(jnp.bfloat16)
-        ctx = jnp.dot(p, v, preferred_element_type=jnp.float32)
-        ctx = jnp.where(valid, ctx, 0.0)
-        o_ref[:, g * HD:(g + 1) * HD] = ctx.astype(o_ref.dtype)
+        o_ref[:, g * HD:(g + 1) * HD] = ctx[g * BLOCK:(g + 1) * BLOCK]
 
 
 def attend(queries, kv_shares, block_image):
@@ -59,6 +60,12 @@
     )(block_image, queries, kv_shares)
 
 
+def holder_of(image_ids, image_slot):
+    image_count = image_slot.shape[0]
+    same_image = image_ids[:, None] == jnp.arange(image_count, dtype=jnp.int32)[None, :]
+    return jnp.sum(jnp.where(same_image, image_slot[None, :], 0), axis=1)
+
+
 def local(queries, memory_kv, block_image, image_slot):
     seq_count = lax.axis_size("seq")
     own_blocks = block_image.shape[0]
@@ -67,10 +74,13 @@
     share_rows = img_rows // ROW_GROUPS
     shares = memory_kv.reshape(ROW_GROUPS, share_rows, kv_local, 2 * HD)
     shares = shares.transpose(0, 2, 1, 3).reshape(seq_count, share_rows, 2 * HD)
-    wanted = lax.all_gather(block_image, "seq", axis=0, tiled=True)
-    held = lax.all_to_all(shares, "seq", split_axis=0, concat_axis=0, tiled=True)
-    wanted_slot = jnp.take(image_slot, jnp.maximum(wanted, 0), axis=0)
-    outgoing = jnp.take(held, wanted_slot, axis=0)
+    tag = jnp.zeros((seq_count, TAG_ROWS, 2 * HD), shares.dtype)
+    tag = tag.at[:, 0, :own_blocks].set(block_image.astype(shares.dtype)[None, :])
+    payload = jnp.concatenate([shares, tag], axis=1)
+    held = lax.all_to_all(payload, "seq", split_axis=0, concat_axis=0, tiled=True)
+    wanted = held[:, share_rows, :own_blocks].astype(jnp.int32).reshape(seq_count * own_blocks)
+    wanted_slot = holder_of(wanted, image_slot)
+    outgoing = jnp.take(held[:, :share_rows], wanted_slot, axis=0, mode="clip")
     outgoing = outgoing.reshape(seq_count, own_blocks, share_rows, 2 * HD)
     arrived = lax.all_to_all(outgoing, "seq", split_axis=0, concat_axis=0, tiled=True)
     arrived = arrived.reshape(ROW_GROUPS, kv_local, own_blocks, share_rows, 2 * HD)

time: 224 us -> 164 us (0.73)
  Pallas kernels: 60 us -> 23.2 us
  other arithmetic: 22.6 us -> 0.95 us
  blocking collectives: 121 us -> 134 us
  starting transfers between devices: 11.3 us -> 0 us
  local copies, waits for them, and re-layouts: 8.42 us -> 5.32 us
    all_to_all x0 -> x1, blocking collectives: none -> 39.2 us  [local(): lax.all_to_all(payload, 'seq', split_axis=0, concat_axis=0, tiled=True)]
    pallas_call x1, Pallas kernels: 60 us -> 23.2 us  [attend(): pl.pallas_call(kernel, grid_spec=grid_spec, out_shape=jax.ShapeDtypeStruc...]
    unnamed x1 -> x0, blocking collectives: 25.3 us -> none
    and x1 -> x0, other arithmetic: 20 us -> none  [local(): outgoing = jnp.take(held, wanted_slot, axis=0)]
    all_to_all x1 -> x0, starting transfers between devices: 11.3 us -> none  [local(): lax.all_to_all(shares, 'seq', split_axis=0, concat_axis=0, tiled=True)]
    select_n x1 -> x0, other arithmetic: 2.54 us -> none  [local(): outgoing = jnp.take(held, wanted_slot, axis=0)]
    gather x3 -> x1, local copies, waits for them, and re-layouts: 4.49 us -> 3.07 us  [local(): outgoing = jnp.take(held[:, :share_rows], wanted_slot, axis=0, mode='clip')]
  transfers between devices with their start and end apart: 1 -> 0, of which waited for: 0 -> 0; matrix products, arithmetic and copies ran while one was open for 10% -> 0% of each run, Pallas kernels for 0% -> 0%
where the time goes in v2:
time: 164 us; the launch traced here: 163 us
  blocking collectives  134 us (82%)
  Pallas kernels  23.2 us (14%)
  local copies, waits for them, and re-layouts  5.32 us (3%)
    all_to_all x1, blocking collectives, local(): lax.all_to_all(outgoing, 'seq', split_axis=0, concat_axis=0, tiled=True)  94.5 us
    all_to_all x1, blocking collectives, local(): lax.all_to_all(payload, 'seq', split_axis=0, concat_axis=0, tiled=True)  39.2 us
    pallas_call x1, Pallas kernels, attend(): pl.pallas_call(kernel, grid_spec=grid_spec, out_shape=jax.ShapeDtypeStruc...  23.2 us

profile of v2, /device:TPU:16, one launch (start us, length us, event | category | flops | bytes accessed | tf_op | source)
XLA Modules:
  0.0 163.3 jit_solution(3879553935734146024)
XLA Ops:
  0.0 0.0 copy-start
  0.0 0.7 convert_bitcast_fusion
  0.7 1.9 %reshape.62 = bf16[8,48,4,256]{3,2,1,0:T(4,128)(2,1)S(1)} reshape(bf16[1,384,1024]{2,1,0:T(8,128)(2,1)} %param.7) | data formatting | bytes 1572864 | tf_op jit(solution)/shard_map/reshape | solution.py:75
  2.6 0.1 copy.6
  2.8 0.1 pad_maximum_fusion
  2.9 39.2 %all_to_all.10 = bf16[32,64,256]{2,1,0:T(8,128)(2,1)S(1)} all-to-all(bf16[32,64,256]{2,1,0:T(8,128)(2,1)S(1)} %pad_maximum_fusion), channel_id=1, replica_groups=mesh['doc'=8,'seq'=32] {'seq'}, dimensions={0} | all-to-all | bytes 2097152 | tf_op jit(solution)/shard_map/all_to_all | solution.py:80
  42.1 0.1 fusion
  42.2 0.1 reshape.67
  42.3 0.0 copy-done
  42.3 0.1 select_reduce_fusion
  42.4 0.1 slice.33
  42.5 3.1 %gather_fusion = bf16[160,48,256]{2,1,0:T(8,128)(2,1)} fusion(bf16[32,48,256]{2,1,0:T(8,128)(2,1)S(1)} %slice.33, s32[1024]{0:T(1024)S(1)} %pad_clamp_fusion), kind=kCustom, calls=%fused_computation | custom fusion | bytes 7864960 | tf_op jit(solution)/shard_map/jit(_take)/gather | solution.py:83
  45.5 94.5 %all_to_all.11 = bf16[32,5,48,256]{3,2,1,0:T(8,128)(2,1)} all-to-all(bf16[32,5,48,256]{3,2,1,0:T(8,128)(2,1)} %bitcast.6), channel_id=1, replica_groups=mesh['doc'=8,'seq'=32] {'seq'}, dimensions={0} | all-to-all | bytes 7864320 | tf_op jit(solution)/shard_map/all_to_all | solution.py:85
  140.1 23.2 %shard_map.46 = bf16[640,4096]{1,0:T(8,128)(2,1)} custom-call(s32[5]{0:T(128)} %image_ref.1, bf16[640,4096]{1,0:T(8,128)(2,1)} %q_ref.1, bf16[8,4,5,48,256]{4,3,2,1,0:T(8,128)(2,1)} %bitcast.7), custom_call_target="tpu_custom_call" | custom-call | tf_op jit(solution)/shard_map/pallas_call | solution.py:56
  (3 shorter events, 0.0 us)
Async XLA Ops:
  0.0 42.3 %copy-start = (s32[32]{0:T(128)S(1)}, s32[32]{0:T(128)}, u32[]{:S(2)}) copy-start(s32[32]{0:T(128)} %param.9) | copy-start | bytes 388

commit v3 on v2

--- a/solution.py
+++ b/solution.py
@@ -12,46 +12,53 @@
 BLOCK = 128
 ROW_GROUPS = 8
 TAG_ROWS = 16
+LOG2E = 1.4426950408889634
 
 
-def attend_kernel(image_ref, q_ref, kv_ref, o_ref, *, group_size, memory_rows):
-    b = pl.program_id(0)
-    kv = kv_ref[...].reshape(memory_rows, 2 * HD)
+def attend_head(q_ref, kv, o_ref, valid, col0, group_size):
     k = kv[:, :HD]
     v = kv[:, HD:]
-    valid = image_ref[b] >= 0
-    q = jnp.concatenate([q_ref[:, g * HD:(g + 1) * HD] for g in range(group_size)], axis=0)
+    q = jnp.concatenate(
+        [q_ref[:, col0 + g * HD:col0 + (g + 1) * HD] for g in range(group_size)], axis=0
+    )
     s = lax.dot_general(k, q, (((1,), (1,)), ((), ())), preferred_element_type=jnp.float32)
-    s = s * HD ** (-0.5)
     m = jnp.max(s, axis=0, keepdims=True)
-    w = jnp.exp(s - m)
+    w = jnp.exp2((s - m) * (HD ** (-0.5) * LOG2E))
     inv = 1.0 / jnp.sum(w, axis=0, keepdims=True)
     p = (w * inv).astype(jnp.bfloat16)
     ctx = lax.dot_general(p, v, (((0,), (0,)), ((), ())), preferred_element_type=jnp.float32)
     ctx = jnp.where(valid, ctx, 0.0).astype(o_ref.dtype)
     for g in range(group_size):
-        o_ref[:, g * HD:(g + 1) * HD] = ctx[g * BLOCK:(g + 1) * BLOCK]
+        o_ref[:, col0 + g * HD:col0 + (g + 1) * HD] = ctx[g * BLOCK:(g + 1) * BLOCK]
+
+
+def attend_kernel(image_ref, q_ref, kv_ref, o_ref, *, group_size, kv_local, memory_rows):
+    b = pl.program_id(0)
+    valid = image_ref[b] >= 0
+    for j in range(kv_local):
+        kv = kv_ref[:, j].reshape(memory_rows, 2 * HD)
+        attend_head(q_ref, kv, o_ref, valid, j * group_size * HD, group_size)
 
 
 def attend(queries, kv_shares, block_image):
     row_count, row_width = queries.shape
     _, kv_local, count_blocks, share_rows, _ = kv_shares.shape
     group_size = row_width // (HD * kv_local)
-    head_cols = group_size * HD
     kernel = functools.partial(
-        attend_kernel, group_size=group_size, memory_rows=ROW_GROUPS * share_rows
+        attend_kernel, group_size=group_size, kv_local=kv_local,
+        memory_rows=ROW_GROUPS * share_rows,
     )
     grid_spec = pltpu.PrefetchScalarGridSpec(
         num_scalar_prefetch=1,
-        grid=(count_blocks, kv_local),
+        grid=(count_blocks,),
         in_specs=[
-            pl.BlockSpec((BLOCK, head_cols), lambda b, j, img: (b, j)),
+            pl.BlockSpec((BLOCK, row_width), lambda b, img: (b, 0)),
             pl.BlockSpec(
-                (ROW_GROUPS, None, None, share_rows, 2 * HD),
-                lambda b, j, img: (0, j, b, 0, 0),
+                (ROW_GROUPS, kv_local, None, share_rows, 2 * HD),
+                lambda b, img: (0, 0, b, 0, 0),
             ),
         ],
-        out_specs=pl.BlockSpec((BLOCK, head_cols), lambda b, j, img: (b, j)),
+        out_specs=pl.BlockSpec((BLOCK, row_width), lambda b, img: (b, 0)),
     )
     return pl.pallas_call(
         kernel,

time: 164 us -> 159 us (0.970)
  Pallas kernels: 23.2 us -> 18.1 us
    pallas_call x1, Pallas kernels: 23.2 us -> 18.1 us  [attend(): pl.pallas_call(kernel, grid_spec=grid_spec, out_shape=jax.ShapeDtypeStruc...]
where the time goes in v3:
time: 159 us; the launch traced here: 158 us
  blocking collectives  134 us (84%)
  Pallas kernels  18.1 us (11%)
  local copies, waits for them, and re-layouts  5.32 us (3%)
    all_to_all x1, blocking collectives, local(): lax.all_to_all(outgoing, 'seq', split_axis=0, concat_axis=0, tiled=True)  94.5 us
    all_to_all x1, blocking collectives, local(): lax.all_to_all(payload, 'seq', split_axis=0, concat_axis=0, tiled=True)  39.2 us
    pallas_call x1, Pallas kernels, attend(): pl.pallas_call(kernel, grid_spec=grid_spec, out_shape=jax.ShapeDtypeStruc...  18.1 us

profile of v3, /device:TPU:16, one launch (start us, length us, event | category | flops | bytes accessed | tf_op | source)
XLA Modules:
  0.0 158.2 jit_solution(5101864360507541959)
XLA Ops:
  0.0 0.0 copy-start
  0.0 0.7 convert_bitcast_fusion
  0.7 1.9 %reshape.62 = bf16[8,48,4,256]{3,2,1,0:T(4,128)(2,1)S(1)} reshape(bf16[1,384,1024]{2,1,0:T(8,128)(2,1)} %param.7) | data formatting | bytes 1572864 | tf_op jit(solution)/shard_map/reshape | solution.py:82
  2.6 0.1 copy.6
  2.8 0.1 pad_maximum_fusion
  2.9 39.2 %all_to_all.10 = bf16[32,64,256]{2,1,0:T(8,128)(2,1)S(1)} all-to-all(bf16[32,64,256]{2,1,0:T(8,128)(2,1)S(1)} %pad_maximum_fusion), channel_id=1, replica_groups=mesh['doc'=8,'seq'=32] {'seq'}, dimensions={0} | all-to-all | bytes 2097152 | tf_op jit(solution)/shard_map/all_to_all | solution.py:87
  42.1 0.1 fusion
  42.2 0.1 reshape.67
  42.3 0.0 copy-done
  42.3 0.1 select_reduce_fusion
  42.4 0.1 slice.33
  42.5 3.1 %gather_fusion = bf16[160,48,256]{2,1,0:T(8,128)(2,1)} fusion(bf16[32,48,256]{2,1,0:T(8,128)(2,1)S(1)} %slice.33, s32[1024]{0:T(1024)S(1)} %pad_clamp_fusion), kind=kCustom, calls=%fused_computation | custom fusion | bytes 7864960 | tf_op jit(solution)/shard_map/jit(_take)/gather | solution.py:90
  45.5 94.5 %all_to_all.11 = bf16[32,5,48,256]{3,2,1,0:T(8,128)(2,1)} all-to-all(bf16[32,5,48,256]{3,2,1,0:T(8,128)(2,1)} %bitcast.6), channel_id=1, replica_groups=mesh['doc'=8,'seq'=32] {'seq'}, dimensions={0} | all-to-all | bytes 7864320 | tf_op jit(solution)/shard_map/all_to_all | solution.py:92
  140.1 18.1 %shard_map.46 = bf16[640,4096]{1,0:T(8,128)(2,1)} custom-call(s32[5]{0:T(128)} %image_ref.1, bf16[640,4096]{1,0:T(8,128)(2,1)} %q_ref.1, bf16[8,4,5,48,256]{4,3,2,1,0:T(8,128)(2,1)} %bitcast.7), custom_call_target="tpu_custom_call" | custom-call | tf_op jit(solution)/shard_map/pallas_call | solution.py:63
  (3 shorter events, 0.0 us)
Async XLA Ops:
  0.0 42.3 %copy-start = (s32[32]{0:T(128)S(1)}, s32[32]{0:T(128)}, u32[]{:S(2)}) copy-start(s32[32]{0:T(128)} %param.9) | copy-start | bytes 388

commit v4 on v3

--- a/solution.py
+++ b/solution.py
@@ -10,14 +10,11 @@
 HD = 128
 KV_HEADS = 4
 BLOCK = 128
-ROW_GROUPS = 8
 TAG_ROWS = 16
 LOG2E = 1.4426950408889634
 
 
-def attend_head(q_ref, kv, o_ref, valid, col0, group_size):
-    k = kv[:, :HD]
-    v = kv[:, HD:]
+def attend_head(q_ref, k, v, o_ref, valid, col0, group_size):
     q = jnp.concatenate(
         [q_ref[:, col0 + g * HD:col0 + (g + 1) * HD] for g in range(group_size)], axis=0
     )
@@ -36,17 +33,18 @@
     b = pl.program_id(0)
     valid = image_ref[b] >= 0
     for j in range(kv_local):
-        kv = kv_ref[:, j].reshape(memory_rows, 2 * HD)
-        attend_head(q_ref, kv, o_ref, valid, j * group_size * HD, group_size)
+        k = kv_ref[j, 0].reshape(memory_rows, HD)
+        v = kv_ref[j, 1].reshape(memory_rows, HD)
+        attend_head(q_ref, k, v, o_ref, valid, j * group_size * HD, group_size)
 
 
 def attend(queries, kv_shares, block_image):
     row_count, row_width = queries.shape
-    _, kv_local, count_blocks, share_rows, _ = kv_shares.shape
+    kv_local, _, row_groups, count_blocks, share_rows, _ = kv_shares.shape
     group_size = row_width // (HD * kv_local)
     kernel = functools.partial(
         attend_kernel, group_size=group_size, kv_local=kv_local,
-        memory_rows=ROW_GROUPS * share_rows,
+        memory_rows=row_groups * share_rows,
     )
     grid_spec = pltpu.PrefetchScalarGridSpec(
         num_scalar_prefetch=1,
@@ -54,8 +52,8 @@
         in_specs=[
             pl.BlockSpec((BLOCK, row_width), lambda b, img: (b, 0)),
             pl.BlockSpec(
-                (ROW_GROUPS, kv_local, None, share_rows, 2 * HD),
-                lambda b, img: (0, 0, b, 0, 0),
+                (kv_local, 2, row_groups, None, share_rows, HD),
+                lambda b, img: (0, 0, 0, b, 0, 0),
             ),
         ],
         out_specs=pl.BlockSpec((BLOCK, row_width), lambda b, img: (b, 0)),
@@ -78,19 +76,20 @@
     own_blocks = block_image.shape[0]
     _, img_rows, kv_width = memory_kv.shape
     kv_local = kv_width // (2 * HD)
-    share_rows = img_rows // ROW_GROUPS
-    shares = memory_kv.reshape(ROW_GROUPS, share_rows, kv_local, 2 * HD)
-    shares = shares.transpose(0, 2, 1, 3).reshape(seq_count, share_rows, 2 * HD)
-    tag = jnp.zeros((seq_count, TAG_ROWS, 2 * HD), shares.dtype)
+    row_groups = seq_count // (2 * kv_local)
+    share_rows = img_rows // row_groups
+    shares = memory_kv.reshape(row_groups, share_rows, kv_local, 2, HD)
+    shares = shares.transpose(2, 3, 0, 1, 4).reshape(seq_count, share_rows, HD)
+    tag = jnp.zeros((seq_count, TAG_ROWS, HD), shares.dtype)
     tag = tag.at[:, 0, :own_blocks].set(block_image.astype(shares.dtype)[None, :])
     payload = jnp.concatenate([shares, tag], axis=1)
     held = lax.all_to_all(payload, "seq", split_axis=0, concat_axis=0, tiled=True)
     wanted = held[:, share_rows, :own_blocks].astype(jnp.int32).reshape(seq_count * own_blocks)
     wanted_slot = holder_of(wanted, image_slot)
     outgoing = jnp.take(held[:, :share_rows], wanted_slot, axis=0, mode="clip")
-    outgoing = outgoing.reshape(seq_count, own_blocks, share_rows, 2 * HD)
+    outgoing = outgoing.reshape(seq_count, own_blocks, share_rows, HD)
     arrived = lax.all_to_all(outgoing, "seq", split_axis=0, concat_axis=0, tiled=True)
-    arrived = arrived.reshape(ROW_GROUPS, kv_local, own_blocks, share_rows, 2 * HD)
+    arrived = arrived.reshape(kv_local, 2, row_groups, own_blocks, share_rows, HD)
     return attend(queries, arrived, block_image)
 
 

time: 159 us -> 156 us (0.981)
  blocking collectives: 134 us -> 131 us
    all_to_all x1, blocking collectives: 39.2 us -> 36.7 us  [local(): lax.all_to_all(payload, 'seq', split_axis=0, concat_axis=0, tiled=True)]
where the time goes in v4:
time: 156 us
  blocking collectives  131 us (84%)
  Pallas kernels  18.2 us (12%)
  local copies, waits for them, and re-layouts  6.07 us (4%)
    all_to_all x1, blocking collectives, local(): lax.all_to_all(outgoing, 'seq', split_axis=0, concat_axis=0, tiled=True)  94.2 us
    all_to_all x1, blocking collectives, local(): lax.all_to_all(payload, 'seq', split_axis=0, concat_axis=0, tiled=True)  36.7 us
    pallas_call x1, Pallas kernels, attend(): pl.pallas_call(kernel, grid_spec=grid_spec, out_shape=jax.ShapeDtypeStruc...  18.2 us
    gather x1, local copies, waits for them, and re-layouts, local(): outgoing = jnp.take(held[:, :share_rows], wanted_slot, axis=0, mode='clip')  3.21 us

profile of v4, /device:TPU:16, one launch (start us, length us, event | category | flops | bytes accessed | tf_op | source)
XLA Modules:
  0.0 156.1 jit_solution(17615964471009611950)
XLA Ops:
  0.0 0.0 copy-start
  0.0 0.7 convert_bitcast_fusion
  0.7 2.6 %reshape.62 = bf16[4,96,4,2,128]{4,3,2,1,0:T(2,128)(2,1)S(1)} reshape(bf16[1,384,1024]{2,1,0:T(8,128)(2,1)} %param.7) | data formatting | bytes 1572864 | tf_op jit(solution)/shard_map/reshape | solution.py:81
  3.2 0.1 copy.6
  3.4 0.1 pad_maximum_fusion
  3.5 36.7 %all_to_all.10 = bf16[32,112,128]{2,1,0:T(8,128)(2,1)S(1)} all-to-all(bf16[32,112,128]{2,1,0:T(8,128)(2,1)S(1)} %pad_maximum_fusion), channel_id=1, replica_groups=mesh['doc'=8,'seq'=32] {'seq'}, dimensions={0} | all-to-all | bytes 1835008 | tf_op jit(solution)/shard_map/all_to_all | solution.py:86
  40.2 0.1 fusion
  40.2 0.1 reshape.67
  40.3 0.0 copy-done
  40.4 0.1 select_reduce_fusion
  40.5 0.1 slice.33
  40.5 3.2 %gather_fusion = bf16[160,96,128]{2,1,0:T(8,128)(2,1)} fusion(bf16[32,96,128]{2,1,0:T(8,128)(2,1)S(1)} %slice.33, s32[1024]{0:T(1024)S(1)} %pad_clamp_fusion), kind=kCustom, calls=%fused_computation | custom fusion | bytes 7864960 | tf_op jit(solution)/shard_map/jit(_take)/gather | solution.py:89
  43.7 94.2 %all_to_all.11 = bf16[32,5,96,128]{3,2,1,0:T(8,128)(2,1)} all-to-all(bf16[32,5,96,128]{3,2,1,0:T(8,128)(2,1)} %bitcast.6), channel_id=1, replica_groups=mesh['doc'=8,'seq'=32] {'seq'}, dimensions={0} | all-to-all | bytes 7864320 | tf_op jit(solution)/shard_map/all_to_all | solution.py:91
  137.9 18.2 %shard_map.46 = bf16[640,4096]{1,0:T(8,128)(2,1)} custom-call(s32[5]{0:T(128)} %image_ref.1, bf16[640,4096]{1,0:T(8,128)(2,1)} %q_ref.1, bf16[4,2,4,5,96,128]{5,4,3,2,1,0:T(8,128)(2,1)} %bitcast.7), custom_call_target="tpu_custom_call" | custom-call | tf_op jit(solution)/shard_map/pallas_call | solution.py:61
  (3 shorter events, 0.0 us)
Async XLA Ops:
  0.0 40.3 %copy-start = (s32[32]{0:T(128)S(1)}, s32[32]{0:T(128)}, u32[]{:S(2)}) copy-start(s32[32]{0:T(128)} %param.9) | copy-start | bytes 388

commit v5 on v4

--- a/solution.py
+++ b/solution.py
@@ -65,6 +65,41 @@
     )(block_image, queries, kv_shares)
 
 
+def pack_kernel(image_ref, kv_ref, out_ref, *, row_groups, share_rows, parts, own_blocks):
+    row = lax.broadcasted_iota(jnp.int32, (TAG_ROWS, HD), 0)
+    lane = lax.broadcasted_iota(jnp.int32, (TAG_ROWS, HD), 1)
+    tag = jnp.zeros((TAG_ROWS, HD), jnp.float32)
+    for i in range(own_blocks):
+        tag = jnp.where((row == 0) & (lane == i), image_ref[i].astype(jnp.float32), tag)
+    tag = tag.astype(out_ref.dtype)
+    for part in range(parts):
+        for rg in range(row_groups):
+            c = part * row_groups + rg
+            out_ref[c, :share_rows, :] = kv_ref[rg * share_rows:(rg + 1) * share_rows, part * HD:(part + 1) * HD]
+            out_ref[c, share_rows:, :] = tag
+
+
+def pack_shares(memory_kv, block_image, row_groups, share_rows):
+    _, img_rows, kv_width = memory_kv.shape
+    parts = kv_width // HD
+    count = parts * row_groups
+    kernel = functools.partial(
+        pack_kernel, row_groups=row_groups, share_rows=share_rows, parts=parts,
+        own_blocks=block_image.shape[0],
+    )
+    grid_spec = pltpu.PrefetchScalarGridSpec(
+        num_scalar_prefetch=1,
+        grid=(1,),
+        in_specs=[pl.BlockSpec((None, img_rows, kv_width), lambda i, img: (0, 0, 0))],
+        out_specs=pl.BlockSpec((count, share_rows + TAG_ROWS, HD), lambda i, img: (0, 0, 0)),
+    )
+    return pl.pallas_call(
+        kernel,
+        grid_spec=grid_spec,
+        out_shape=jax.ShapeDtypeStruct((count, share_rows + TAG_ROWS, HD), memory_kv.dtype),
+    )(block_image, memory_kv)
+
+
 def holder_of(image_ids, image_slot):
     image_count = image_slot.shape[0]
     same_image = image_ids[:, None] == jnp.arange(image_count, dtype=jnp.int32)[None, :]
@@ -78,11 +113,7 @@
     kv_local = kv_width // (2 * HD)
     row_groups = seq_count // (2 * kv_local)
     share_rows = img_rows // row_groups
-    shares = memory_kv.reshape(row_groups, share_rows, kv_local, 2, HD)
-    shares = shares.transpose(2, 3, 0, 1, 4).reshape(seq_count, share_rows, HD)
-    tag = jnp.zeros((seq_count, TAG_ROWS, HD), shares.dtype)
-    tag = tag.at[:, 0, :own_blocks].set(block_image.astype(shares.dtype)[None, :])
-    payload = jnp.concatenate([shares, tag], axis=1)
+    payload = pack_shares(memory_kv, block_image, row_groups, share_rows)
     held = lax.all_to_all(payload, "seq", split_axis=0, concat_axis=0, tiled=True)
     wanted = held[:, share_rows, :own_blocks].astype(jnp.int32).reshape(seq_count * own_blocks)
     wanted_slot = holder_of(wanted, image_slot)

time: 156 us -> 157 us (level)
  Pallas kernels: 18.2 us -> 21 us
  local copies, waits for them, and re-layouts: 6.07 us -> 3.37 us
    pallas_call x0 -> x1, Pallas kernels: none -> 2.86 us  [pack_shares(): pl.pallas_call(kernel, grid_spec=grid_spec, out_shape=jax.ShapeDtypeStruc...]
    reshape x1 -> x0, local copies, waits for them, and re-layouts: 2.55 us -> none  [local(): shares = memory_kv.reshape(row_groups, share_rows, kv_local, 2, HD)]
where the time goes in v5:
time: 157 us; the launch traced here: 156 us
  blocking collectives  131 us (83%)
  Pallas kernels  21 us (13%)
  local copies, waits for them, and re-layouts  3.37 us (2%)
    all_to_all x1, blocking collectives, local(): lax.all_to_all(outgoing, 'seq', split_axis=0, concat_axis=0, tiled=True)  94.2 us
    all_to_all x1, blocking collectives, local(): lax.all_to_all(payload, 'seq', split_axis=0, concat_axis=0, tiled=True)  36.9 us
    pallas_call x1, Pallas kernels, attend(): pl.pallas_call(kernel, grid_spec=grid_spec, out_shape=jax.ShapeDtypeStruc...  18.2 us
    gather x1, local copies, waits for them, and re-layouts, local(): outgoing = jnp.take(held[:, :share_rows], wanted_slot, axis=0, mode='clip')  3.21 us

profile of v5, /device:TPU:16, one launch (start us, length us, event | category | flops | bytes accessed | tf_op | source)
XLA Modules:
  0.0 156.3 jit_solution(14091774737899167926)
XLA Ops:
  0.0 2.9 %shard_map.46 = bf16[32,112,128]{2,1,0:T(8,128)(2,1)} custom-call(s32[5]{0:T(128)} %image_ref.3, bf16[1,384,1024]{2,1,0:T(8,128)(2,1)} %kv_ref.1), custom_call_target="tpu_custom_call" | custom-call | tf_op jit(solution)/shard_map/pallas_call | solution.py:96
  2.9 36.9 %all_to_all.10 = bf16[32,112,128]{2,1,0:T(8,128)(2,1)S(1)} all-to-all(bf16[32,112,128]{2,1,0:T(8,128)(2,1)} %shard_map.46), channel_id=1, replica_groups=mesh['doc'=8,'seq'=32] {'seq'}, dimensions={0} | all-to-all | bytes 1835008 | tf_op jit(solution)/shard_map/all_to_all | solution.py:117
  39.8 0.1 fusion
  39.8 0.1 reshape.16
  39.9 0.7 select_reduce_fusion
  40.7 0.1 slice.10
  40.8 3.2 %gather_fusion = bf16[160,96,128]{2,1,0:T(8,128)(2,1)} fusion(bf16[32,96,128]{2,1,0:T(8,128)(2,1)S(1)} %slice.10, s32[1024]{0:T(1024)S(1)} %pad_clamp_fusion), kind=kCustom, calls=%fused_computation | custom fusion | bytes 7864960 | tf_op jit(solution)/shard_map/jit(_take)/gather | solution.py:120
  44.0 94.2 %all_to_all.11 = bf16[32,5,96,128]{3,2,1,0:T(8,128)(2,1)} all-to-all(bf16[32,5,96,128]{3,2,1,0:T(8,128)(2,1)} %bitcast.2), channel_id=1, replica_groups=mesh['doc'=8,'seq'=32] {'seq'}, dimensions={0} | all-to-all | bytes 7864320 | tf_op jit(solution)/shard_map/all_to_all | solution.py:122
  138.1 18.2 %shard_map.47 = bf16[640,4096]{1,0:T(8,128)(2,1)} custom-call(s32[5]{0:T(128)} %image_ref.3, bf16[640,4096]{1,0:T(8,128)(2,1)} %q_ref.1, bf16[4,2,4,5,96,128]{5,4,3,2,1,0:T(8,128)(2,1)} %bitcast.3), custom_call_target="tpu_custom_call" | custom-call | tf_op jit(solution)/shard_map/pallas_call | solution.py:61
  (1 shorter events, 0.0 us)

commit v6 on v4

--- a/solution.py
+++ b/solution.py
@@ -29,8 +29,9 @@
         o_ref[:, col0 + g * HD:col0 + (g + 1) * HD] = ctx[g * BLOCK:(g + 1) * BLOCK]
 
 
-def attend_kernel(image_ref, q_ref, kv_ref, o_ref, *, group_size, kv_local, memory_rows):
-    b = pl.program_id(0)
+def attend_kernel(image_ref, q_ref, kv_ref, *refs, group_size, kv_local, memory_rows, first):
+    o_ref = refs[-1]
+    b = pl.program_id(0) + first
     valid = image_ref[b] >= 0
     for j in range(kv_local):
         k = kv_ref[j, 0].reshape(memory_rows, HD)
@@ -38,31 +39,39 @@
         attend_head(q_ref, k, v, o_ref, valid, j * group_size * HD, group_size)
 
 
-def attend(queries, kv_shares, block_image):
+def attend(queries, kv_shares, block_image, first, previous=None):
     row_count, row_width = queries.shape
     kv_local, _, row_groups, count_blocks, share_rows, _ = kv_shares.shape
     group_size = row_width // (HD * kv_local)
     kernel = functools.partial(
         attend_kernel, group_size=group_size, kv_local=kv_local,
-        memory_rows=row_groups * share_rows,
+        memory_rows=row_groups * share_rows, first=first,
     )
+    in_specs = [
+        pl.BlockSpec((BLOCK, row_width), lambda b, img: (b + first, 0)),
+        pl.BlockSpec(
+            (kv_local, 2, row_groups, None, share_rows, HD),
+            lambda b, img: (0, 0, 0, b, 0, 0),
+        ),
+    ]
+    operands = [block_image, queries, kv_shares]
+    aliases = {}
+    if previous is not None:
+        in_specs.append(pl.BlockSpec(memory_space=pl.ANY))
+        operands.append(previous)
+        aliases = {3: 0}
     grid_spec = pltpu.PrefetchScalarGridSpec(
         num_scalar_prefetch=1,
         grid=(count_blocks,),
-        in_specs=[
-            pl.BlockSpec((BLOCK, row_width), lambda b, img: (b, 0)),
-            pl.BlockSpec(
-                (kv_local, 2, row_groups, None, share_rows, HD),
-                lambda b, img: (0, 0, 0, b, 0, 0),
-            ),
-        ],
-        out_specs=pl.BlockSpec((BLOCK, row_width), lambda b, img: (b, 0)),
+        in_specs=in_specs,
+        out_specs=pl.BlockSpec((BLOCK, row_width), lambda b, img: (b + first, 0)),
     )
     return pl.pallas_call(
         kernel,
         grid_spec=grid_spec,
         out_shape=jax.ShapeDtypeStruct(queries.shape, queries.dtype),
-    )(block_image, queries, kv_shares)
+        input_output_aliases=aliases,
+    )(*operands)
 
 
 def holder_of(image_ids, image_slot):
@@ -88,9 +97,13 @@
     wanted_slot = holder_of(wanted, image_slot)
     outgoing = jnp.take(held[:, :share_rows], wanted_slot, axis=0, mode="clip")
     outgoing = outgoing.reshape(seq_count, own_blocks, share_rows, HD)
-    arrived = lax.all_to_all(outgoing, "seq", split_axis=0, concat_axis=0, tiled=True)
-    arrived = arrived.reshape(kv_local, 2, row_groups, own_blocks, share_rows, HD)
-    return attend(queries, arrived, block_image)
+    split = own_blocks - 1
+    early = lax.all_to_all(outgoing[:, :split], "seq", split_axis=0, concat_axis=0, tiled=True)
+    late = lax.all_to_all(outgoing[:, split:], "seq", split_axis=0, concat_axis=0, tiled=True)
+    early = early.reshape(kv_local, 2, row_groups, split, share_rows, HD)
+    late = late.reshape(kv_local, 2, row_groups, own_blocks - split, share_rows, HD)
+    result = attend(queries, early, block_image, 0)
+    return attend(queries, late, block_image, split, result)
 
 
 def solution(mesh):

time: 156 us -> 158 us (1.013)
  blocking collectives: 131 us -> 36.7 us
  waiting for transfers between devices: 0 us -> 75.1 us
  starting transfers between devices: 0 us -> 11.6 us
  local copies, waits for them, and re-layouts: 6.07 us -> 12 us
  Pallas kernels: 18.2 us -> 21.2 us
    all_to_all x1 -> x0, blocking collectives: 94.2 us -> none  [local(): lax.all_to_all(outgoing, 'seq', split_axis=0, concat_axis=0, tiled=True)]
    all_to_all x0 -> x2, waiting for transfers between devices: none -> 75.1 us  [the longest x1 69 us: local(): lax.all_to_all(outgoing[:, :split], 'seq', split_axis=0, concat_axis=0, t...]
    all_to_all x0 -> x2, starting transfers between devices: none -> 11.6 us  [the longest x1 6.4 us: local(): lax.all_to_all(outgoing[:, split:], 'seq', split_axis=0, concat_axis=0, t...]
    slice x0 -> x2, local copies, waits for them, and re-layouts: none -> 5.97 us  [the longest x1 3.9 us: local(): outgoing[:, :split]]
    pallas_call x1 -> x2, Pallas kernels: 18.2 us -> 21.2 us  [attend(): pl.pallas_call(kernel, grid_spec=grid_spec, out_shape=jax.ShapeDtypeStruc...]
  transfers between devices with their start and end apart: 0 -> 2, of which waited for: 0 -> 2; matrix products, arithmetic and copies ran while one was open for 0% -> 1% of each run, Pallas kernels for 0% -> 10%
where the time goes in v6:
time: 158 us
  waiting for transfers between devices  75.1 us (48%)
  blocking collectives  36.7 us (23%)
  Pallas kernels  21.2 us (13%)
  local copies, waits for them, and re-layouts  12 us (8%)
  starting transfers between devices  11.6 us (7%)
    all_to_all x1, waiting for transfers between devices, local(): lax.all_to_all(outgoing[:, :split], 'seq', split_axis=0, concat_axis=0, t...  69 us
    all_to_all x1, blocking collectives, local(): lax.all_to_all(payload, 'seq', split_axis=0, concat_axis=0, tiled=True)  36.7 us
    pallas_call x2, Pallas kernels, attend(): pl.pallas_call(kernel, grid_spec=grid_spec, out_shape=jax.ShapeDtypeStruc...  21.2 us
    all_to_all x1, starting transfers between devices, local(): lax.all_to_all(outgoing[:, split:], 'seq', split_axis=0, concat_axis=0, t...  6.4 us
    all_to_all x1, waiting for transfers between devices, local(): lax.all_to_all(outgoing[:, split:], 'seq', split_axis=0, concat_axis=0, t...  6.09 us
    all_to_all x1, starting transfers between devices, local(): lax.all_to_all(outgoing[:, :split], 'seq', split_axis=0, concat_axis=0, t...  5.23 us
    slice x1, local copies, waits for them, and re-layouts, local(): outgoing[:, :split]  3.9 us
    gather x1, local copies, waits for them, and re-layouts, local(): outgoing = jnp.take(held[:, :share_rows], wanted_slot, axis=0, mode='clip')  3.21 us
  transfers between devices with their start and end apart: 2, of which 2 were waited for; matrix products, arithmetic and copies ran while one was open for 1% of the time, Pallas kernels for 10%

profile of v6, /device:TPU:16, one launch (start us, length us, event | category | flops | bytes accessed | tf_op | source)
XLA Modules:
  0.0 157.7 jit_solution(4427457834649593539)
XLA Ops:
  0.0 0.0 copy-start.1
  0.0 0.7 convert_bitcast_fusion
  0.7 2.6 %reshape.65 = bf16[4,96,4,2,128]{4,3,2,1,0:T(2,128)(2,1)S(1)} reshape(bf16[1,384,1024]{2,1,0:T(8,128)(2,1)} %param.7) | data formatting | bytes 1572864 | tf_op jit(solution)/shard_map/reshape | solution.py:90
  3.2 0.1 copy.8
  3.4 0.1 pad_maximum_fusion
  3.5 36.7 %all_to_all.15 = bf16[32,112,128]{2,1,0:T(8,128)(2,1)S(1)} all-to-all(bf16[32,112,128]{2,1,0:T(8,128)(2,1)S(1)} %pad_maximum_fusion), channel_id=1, replica_groups=mesh['doc'=8,'seq'=32] {'seq'}, dimensions={0} | all-to-all | bytes 1835008 | tf_op jit(solution)/shard_map/all_to_all | solution.py:95
  40.2 0.1 fusion
  40.2 0.1 reshape.71
  40.3 0.0 copy-done.1
  40.4 0.1 select_reduce_fusion
  40.5 0.1 slice.41
  40.5 3.2 %gather_fusion = bf16[160,96,128]{2,1,0:T(8,128)(2,1)} fusion(bf16[32,96,128]{2,1,0:T(8,128)(2,1)S(1)} %slice.41, s32[1024]{0:T(1024)S(1)} %pad_clamp_fusion), kind=kCustom, calls=%fused_computation | custom fusion | bytes 7864960 | tf_op jit(solution)/shard_map/jit(_take)/gather | solution.py:98
  43.7 3.9 %slice.44 = bf16[32,4,96,128]{3,2,1,0:T(8,128)(2,1)} slice(bf16[32,5,96,128]{3,2,1,0:T(8,128)(2,1)} %bitcast.7), slice={[0:32], [0:4], [0:96], [0:128]} | slice | bytes 6291456 | tf_op jit(solution)/shard_map/slice | solution.py:101
  47.6 5.2 %all-to-all-start.2 = ((bf16[32,4,96,128]{3,2,1,0:T(8,128)(2,1)}), bf16[32,4,96,128]{3,2,1,0:T(8,128)(2,1)S(1)}, u32[]{:S(2)}, u32[]{:S(2)}) async-start(bf16[32,4,96,128]{3,2,1,0:T(8,128)(2,1)} %slice.44), calls=%async_computation.2 | async-start | bytes 6291456 | tf_op jit(solution)/shard_map/all_to_all | solution.py:101
  52.9 2.1 %slice.43 = bf16[32,1,96,128]{3,2,1,0:T(8,128)(2,1)} slice(bf16[32,5,96,128]{3,2,1,0:T(8,128)(2,1)} %bitcast.8), slice={[0:32], [4:5], [0:96], [0:128]} | slice | bytes 1572864 | tf_op jit(solution)/shard_map/slice | solution.py:102
  54.9 69.0 %all-to-all-done.2 = bf16[32,4,96,128]{3,2,1,0:T(8,128)(2,1)S(1)} async-done(((bf16[32,4,96,128]{3,2,1,0:T(8,128)(2,1)}), bf16[32,4,96,128]{3,2,1,0:T(8,128)(2,1)S(1)}, u32[]{:S(2)}, u32[]{:S(2)}) %all-to-all-start.2) | async-done | bytes 3145760 | tf_op jit(solution)/shard_map/all_to_all | solution.py:101
  123.9 0.0 copy-start
  123.9 6.4 %all-to-all-start.1 = ((bf16[32,1,96,128]{3,2,1,0:T(8,128)(2,1)}), bf16[32,1,96,128]{3,2,1,0:T(8,128)(2,1)}, u32[]{:S(2)}, u32[]{:S(2)}) async-start(bf16[32,1,96,128]{3,2,1,0:T(8,128)(2,1)} %slice.43), calls=%async_computation.1 | async-start | bytes 1572864 | tf_op jit(solution)/shard_map/all_to_all | solution.py:102
  130.3 0.0 copy-done
  130.4 15.2 %shard_map.46.refs_0_ = bf16[640,4096]{1,0:T(8,128)(2,1)} custom-call(s32[5]{0:T(128)} %image_ref.3, bf16[640,4096]{1,0:T(8,128)(2,1)} %q_ref.3, bf16[4,2,4,4,96,128]{5,4,3,2,1,0:T(8,128)(2,1)} %bitcast.9), custom_call_target="tpu_custom_call" | custom-call | tf_op jit(solution)/shard_map/pallas_call | solution.py:69
  145.5 6.1 %all-to-all-done.1 = bf16[32,1,96,128]{3,2,1,0:T(8,128)(2,1)} async-done(((bf16[32,1,96,128]{3,2,1,0:T(8,128)(2,1)}), bf16[32,1,96,128]{3,2,1,0:T(8,128)(2,1)}, u32[]{:S(2)}, u32[]{:S(2)}) %all-to-all-start.1) | async-done | bytes 786464 | tf_op jit(solution)/shard_map/all_to_all | solution.py:102
  151.6 6.1 %shard_map.47 = bf16[640,4096]{1,0:T(8,128)(2,1)} custom-call(s32[5]{0:T(128)} %image_ref.3, bf16[640,4096]{1,0:T(8,128)(2,1)} %q_ref.3, bf16[4,2,4,1,96,128]{5,4,3,2,1,0:T(8,128)(2,1)} %bitcast.4.kv_ref, bf16[640,4096]{1,0:T(8,128)(2,1)} %shard_map.46.refs_0_), custom_call_target="tpu_custom_call", output_to_operand_aliasing={{}: (3, {})} | custom-call | tf_op jit(solution)/shard_map/pallas_call | solution.py:69
  (3 shorter events, 0.0 us)
Async XLA Ops:
  0.0 40.3 %copy-start.1 = (s32[32]{0:T(128)S(1)}, s32[32]{0:T(128)}, u32[]{:S(2)}) copy-start(s32[32]{0:T(128)} %param.9) | copy-start | bytes 388
  47.6 76.3 %all-to-all-start.2 = ((bf16[32,4,96,128]{3,2,1,0:T(8,128)(2,1)}), bf16[32,4,96,128]{3,2,1,0:T(8,128)(2,1)S(1)}, u32[]{:S(2)}, u32[]{:S(2)}) async-start(bf16[32,4,96,128]{3,2,1,0:T(8,128)(2,1)} %slice.44), calls=%async_computation.2 | async-start | bytes 6291456 | tf_op jit(solution)/shard_map/all_to_all | solution.py:101
  123.9 6.4 %copy-start = (bf16[32,4,96,128]{3,2,1,0:T(8,128)(2,1)}, bf16[32,4,96,128]{3,2,1,0:T(8,128)(2,1)S(1)}, u32[]{:S(2)}) copy-start(bf16[32,4,96,128]{3,2,1,0:T(8,128)(2,1)S(1)} %all-to-all-done.2) | copy-start | bytes 9437188
  123.9 27.7 %all-to-all-start.1 = ((bf16[32,1,96,128]{3,2,1,0:T(8,128)(2,1)}), bf16[32,1,96,128]{3,2,1,0:T(8,128)(2,1)}, u32[]{:S(2)}, u32[]{:S(2)}) async-start(bf16[32,1,96,128]{3,2,1,0:T(8,128)(2,1)} %slice.43), calls=%async_computation.1 | async-start | bytes 1572864 | tf_op jit(solution)/shard_map/all_to_all | solution.py:102

commit v7 on v6

--- a/solution.py
+++ b/solution.py
@@ -95,11 +95,15 @@
     held = lax.all_to_all(payload, "seq", split_axis=0, concat_axis=0, tiled=True)
     wanted = held[:, share_rows, :own_blocks].astype(jnp.int32).reshape(seq_count * own_blocks)
     wanted_slot = holder_of(wanted, image_slot)
-    outgoing = jnp.take(held[:, :share_rows], wanted_slot, axis=0, mode="clip")
-    outgoing = outgoing.reshape(seq_count, own_blocks, share_rows, HD)
     split = own_blocks - 1
-    early = lax.all_to_all(outgoing[:, :split], "seq", split_axis=0, concat_axis=0, tiled=True)
-    late = lax.all_to_all(outgoing[:, split:], "seq", split_axis=0, concat_axis=0, tiled=True)
+    wanted_slot = wanted_slot.reshape(seq_count, own_blocks)
+    source = held[:, :share_rows]
+    early = jnp.take(source, wanted_slot[:, :split].reshape(-1), axis=0, mode="clip")
+    late = jnp.take(source, wanted_slot[:, split:].reshape(-1), axis=0, mode="clip")
+    early = early.reshape(seq_count, split, share_rows, HD)
+    late = late.reshape(seq_count, own_blocks - split, share_rows, HD)
+    early = lax.all_to_all(early, "seq", split_axis=0, concat_axis=0, tiled=True)
+    late = lax.all_to_all(late, "seq", split_axis=0, concat_axis=0, tiled=True)
     early = early.reshape(kv_local, 2, row_groups, split, share_rows, HD)
     late = late.reshape(kv_local, 2, row_groups, own_blocks - split, share_rows, HD)
     result = attend(queries, early, block_image, 0)

time: 158 us -> 155 us (0.981)
  local copies, waits for them, and re-layouts: 12 us -> 8.28 us
    slice x3 -> x2, local copies, waits for them, and re-layouts: 6.03 us -> 0.23 us  [the longest x1 0.18 us: local(): wanted_slot[:, split:].reshape(-1)]
    gather x1 -> x2, local copies, waits for them, and re-layouts: 3.21 us -> 4.15 us  [the longest x1 2.61 us: local(): jnp.take(source, wanted_slot[:, :split].reshape(-1), axis=0, mode='clip')]
where the time goes in v7:
time: 155 us; the launch traced here: 154 us
  waiting for transfers between devices  75.4 us (49%)
  blocking collectives  36.7 us (24%)
  Pallas kernels  21.2 us (14%)
  starting transfers between devices  11.6 us (7%)
  local copies, waits for them, and re-layouts  8.28 us (5%)
    all_to_all x1, waiting for transfers between devices, local(): lax.all_to_all(early, 'seq', split_axis=0, concat_axis=0, tiled=True)  69.3 us
    all_to_all x1, blocking collectives, local(): lax.all_to_all(payload, 'seq', split_axis=0, concat_axis=0, tiled=True)  36.7 us
    pallas_call x2, Pallas kernels, attend(): pl.pallas_call(kernel, grid_spec=grid_spec, out_shape=jax.ShapeDtypeStruc...  21.2 us
    all_to_all x1, starting transfers between devices, local(): late = lax.all_to_all(late, 'seq', split_axis=0, concat_axis=0, tiled=True)  6.29 us
    all_to_all x1, waiting for transfers between devices, local(): late = lax.all_to_all(late, 'seq', split_axis=0, concat_axis=0, tiled=True)  6.12 us
    all_to_all x1, starting transfers between devices, local(): lax.all_to_all(early, 'seq', split_axis=0, concat_axis=0, tiled=True)  5.34 us
  transfers between devices with their start and end apart: 2, of which 2 were waited for; matrix products, arithmetic and copies ran while one was open for 1% of the time, Pallas kernels for 10%

profile of v7, /device:TPU:16, one launch (start us, length us, event | category | flops | bytes accessed | tf_op | source)
XLA Modules:
  0.0 154.3 jit_solution(8489444569371447212)
XLA Ops:
  0.0 0.7 convert_bitcast_fusion
  0.7 0.0 copy-start.1
  0.7 2.6 %reshape.74 = bf16[4,96,4,2,128]{4,3,2,1,0:T(2,128)(2,1)S(1)} reshape(bf16[1,384,1024]{2,1,0:T(8,128)(2,1)} %param.7) | data formatting | bytes 1572864 | tf_op jit(solution)/shard_map/reshape | solution.py:90
  3.2 0.1 copy.9
  3.4 0.1 pad_maximum_fusion
  3.5 36.7 %all_to_all.15 = bf16[32,112,128]{2,1,0:T(8,128)(2,1)S(1)} all-to-all(bf16[32,112,128]{2,1,0:T(8,128)(2,1)S(1)} %pad_maximum_fusion), channel_id=1, replica_groups=mesh['doc'=8,'seq'=32] {'seq'}, dimensions={0} | all-to-all | bytes 1835008 | tf_op jit(solution)/shard_map/all_to_all | solution.py:95
  40.2 0.1 fusion
  40.2 0.1 reshape.82
  40.3 0.0 copy-done.1
  40.4 0.1 select_reduce_fusion
  40.4 0.1 reshape.77
  40.5 0.1 reshape.93
  40.7 0.1 slice.43
  40.7 2.6 %gather_fusion.1 = bf16[128,96,128]{2,1,0:T(8,128)(2,1)} fusion(bf16[32,96,128]{2,1,0:T(8,128)(2,1)S(1)} %slice.43, s32[1024]{0:T(1024)S(1)} %pad_clamp_fusion), kind=kCustom, calls=%fused_computation.1 | custom fusion | bytes 6291968 | tf_op jit(solution)/shard_map/jit(_take)/gather | solution.py:101
  43.4 5.3 %all-to-all-start.2 = ((bf16[32,4,96,128]{3,2,1,0:T(8,128)(2,1)}), bf16[32,4,96,128]{3,2,1,0:T(8,128)(2,1)}, u32[]{:S(2)}, u32[]{:S(2)}) async-start(bf16[32,4,96,128]{3,2,1,0:T(8,128)(2,1)} %bitcast.11), calls=%async_computation.2 | async-start | bytes 6291456 | tf_op jit(solution)/shard_map/all_to_all | solution.py:105
  48.7 0.2 slice_reduce_fusion
  48.9 1.5 gather_fusion
  50.4 69.3 %all-to-all-done.2 = bf16[32,4,96,128]{3,2,1,0:T(8,128)(2,1)} async-done(((bf16[32,4,96,128]{3,2,1,0:T(8,128)(2,1)}), bf16[32,4,96,128]{3,2,1,0:T(8,128)(2,1)}, u32[]{:S(2)}, u32[]{:S(2)}) %all-to-all-start.2) | async-done | bytes 3145760 | tf_op jit(solution)/shard_map/all_to_all | solution.py:105
  119.8 6.3 %all-to-all-start.1 = ((bf16[32,1,96,128]{3,2,1,0:T(8,128)(2,1)}), bf16[32,1,96,128]{3,2,1,0:T(8,128)(2,1)S(1)}, u32[]{:S(2)}, u32[]{:S(2)}) async-start(bf16[32,1,96,128]{3,2,1,0:T(8,128)(2,1)} %bitcast.4), calls=%async_computation.1 | async-start | bytes 1572864 | tf_op jit(solution)/shard_map/all_to_all | solution.py:106
  126.1 15.2 %shard_map.46.refs_0_ = bf16[640,4096]{1,0:T(8,128)(2,1)} custom-call(s32[5]{0:T(128)} %image_ref.3, bf16[640,4096]{1,0:T(8,128)(2,1)} %q_ref.3, bf16[4,2,4,4,96,128]{5,4,3,2,1,0:T(8,128)(2,1)} %bitcast.7.kv_ref), custom_call_target="tpu_custom_call" | custom-call | tf_op jit(solution)/shard_map/pallas_call | solution.py:69
  141.2 6.1 %all-to-all-done.1 = bf16[32,1,96,128]{3,2,1,0:T(8,128)(2,1)S(1)} async-done(((bf16[32,1,96,128]{3,2,1,0:T(8,128)(2,1)}), bf16[32,1,96,128]{3,2,1,0:T(8,128)(2,1)S(1)}, u32[]{:S(2)}, u32[]{:S(2)}) %all-to-all-start.1) | async-done | bytes 786464 | tf_op jit(solution)/shard_map/all_to_all | solution.py:106
  147.3 0.0 copy-start
  147.3 0.9 copy-done
  148.2 6.1 %shard_map.47 = bf16[640,4096]{1,0:T(8,128)(2,1)} custom-call(s32[5]{0:T(128)} %image_ref.3, bf16[640,4096]{1,0:T(8,128)(2,1)} %q_ref.3, bf16[4,2,4,1,96,128]{5,4,3,2,1,0:T(8,128)(2,1)} %bitcast.12, bf16[640,4096]{1,0:T(8,128)(2,1)} %shard_map.46.refs_0_), custom_call_target="tpu_custom_call", output_to_operand_aliasing={{}: (3, {})} | custom-call | tf_op jit(solution)/shard_map/pallas_call | solution.py:69
  (4 shorter events, 0.0 us)
Async XLA Ops:
  0.7 39.7 %copy-start.1 = (s32[32]{0:T(128)S(1)}, s32[32]{0:T(128)}, u32[]{:S(2)}) copy-start(s32[32]{0:T(128)} %param.9) | copy-start | bytes 388
  43.4 76.4 %all-to-all-start.2 = ((bf16[32,4,96,128]{3,2,1,0:T(8,128)(2,1)}), bf16[32,4,96,128]{3,2,1,0:T(8,128)(2,1)}, u32[]{:S(2)}, u32[]{:S(2)}) async-start(bf16[32,4,96,128]{3,2,1,0:T(8,128)(2,1)} %bitcast.11), calls=%async_computation.2 | async-start | bytes 6291456 | tf_op jit(solution)/shard_map/all_to_all | solution.py:105
  119.8 27.6 %all-to-all-start.1 = ((bf16[32,1,96,128]{3,2,1,0:T(8,128)(2,1)}), bf16[32,1,96,128]{3,2,1,0:T(8,128)(2,1)S(1)}, u32[]{:S(2)}, u32[]{:S(2)}) async-start(bf16[32,1,96,128]{3,2,1,0:T(8,128)(2,1)} %bitcast.4), calls=%async_computation.1 | async-start | bytes 1572864 | tf_op jit(solution)/shard_map/all_to_all | solution.py:106
  147.3 0.9 copy-start

commit v8 on v7

--- a/solution.py
+++ b/solution.py
@@ -39,19 +39,20 @@
         attend_head(q_ref, k, v, o_ref, valid, j * group_size * HD, group_size)
 
 
-def attend(queries, kv_shares, block_image, first, previous=None):
+def attend(queries, kv_shares, block_image, first, heads_per_step, previous=None):
     row_count, row_width = queries.shape
     kv_local, _, row_groups, count_blocks, share_rows, _ = kv_shares.shape
     group_size = row_width // (HD * kv_local)
+    step_cols = heads_per_step * group_size * HD
     kernel = functools.partial(
-        attend_kernel, group_size=group_size, kv_local=kv_local,
+        attend_kernel, group_size=group_size, kv_local=heads_per_step,
         memory_rows=row_groups * share_rows, first=first,
     )
     in_specs = [
-        pl.BlockSpec((BLOCK, row_width), lambda b, img: (b + first, 0)),
+        pl.BlockSpec((BLOCK, step_cols), lambda b, h, img: (b + first, h)),
         pl.BlockSpec(
-            (kv_local, 2, row_groups, None, share_rows, HD),
-            lambda b, img: (0, 0, 0, b, 0, 0),
+            (heads_per_step, 2, row_groups, None, share_rows, HD),
+            lambda b, h, img: (h, 0, 0, b, 0, 0),
         ),
     ]
     operands = [block_image, queries, kv_shares]
@@ -62,9 +63,9 @@
         aliases = {3: 0}
     grid_spec = pltpu.PrefetchScalarGridSpec(
         num_scalar_prefetch=1,
-        grid=(count_blocks,),
+        grid=(count_blocks, kv_local // heads_per_step),
         in_specs=in_specs,
-        out_specs=pl.BlockSpec((BLOCK, row_width), lambda b, img: (b + first, 0)),
+        out_specs=pl.BlockSpec((BLOCK, step_cols), lambda b, h, img: (b + first, h)),
     )
     return pl.pallas_call(
         kernel,
@@ -106,8 +107,8 @@
     late = lax.all_to_all(late, "seq", split_axis=0, concat_axis=0, tiled=True)
     early = early.reshape(kv_local, 2, row_groups, split, share_rows, HD)
     late = late.reshape(kv_local, 2, row_groups, own_blocks - split, share_rows, HD)
-    result = attend(queries, early, block_image, 0)
-    return attend(queries, late, block_image, split, result)
+    result = attend(queries, early, block_image, 0, kv_local)
+    return attend(queries, late, block_image, split, 1, result)
 
 
 def solution(mesh):

time: 155 us -> 155 us (level)
  no operation moved by 1% of the time
where the time goes in v8:
time: 155 us; the launch traced here: 154 us
  waiting for transfers between devices  75.4 us (49%)
  blocking collectives  36.7 us (24%)
  Pallas kernels  21.3 us (14%)
  starting transfers between devices  11.6 us (7%)
  local copies, waits for them, and re-layouts  8.28 us (5%)
    all_to_all x1, waiting for transfers between devices, local(): lax.all_to_all(early, 'seq', split_axis=0, concat_axis=0, tiled=True)  69.3 us
    all_to_all x1, blocking collectives, local(): lax.all_to_all(payload, 'seq', split_axis=0, concat_axis=0, tiled=True)  36.7 us
    pallas_call x2, Pallas kernels, attend(): pl.pallas_call(kernel, grid_spec=grid_spec, out_shape=jax.ShapeDtypeStruc...  21.3 us
    all_to_all x1, starting transfers between devices, local(): late = lax.all_to_all(late, 'seq', split_axis=0, concat_axis=0, tiled=True)  6.29 us
    all_to_all x1, waiting for transfers between devices, local(): late = lax.all_to_all(late, 'seq', split_axis=0, concat_axis=0, tiled=True)  6.12 us
    all_to_all x1, starting transfers between devices, local(): lax.all_to_all(early, 'seq', split_axis=0, concat_axis=0, tiled=True)  5.34 us
  transfers between devices with their start and end apart: 2, of which 2 were waited for; matrix products, arithmetic and copies ran while one was open for 1% of the time, Pallas kernels for 10%

profile of v8, /device:TPU:16, one launch (start us, length us, event | category | flops | bytes accessed | tf_op | source)
XLA Modules:
  0.0 154.4 jit_solution(1806673971627976270)
XLA Ops:
  0.0 0.7 convert_bitcast_fusion
  0.7 0.0 copy-start.1
  0.7 2.6 %reshape.74 = bf16[4,96,4,2,128]{4,3,2,1,0:T(2,128)(2,1)S(1)} reshape(bf16[1,384,1024]{2,1,0:T(8,128)(2,1)} %param.7) | data formatting | bytes 1572864 | tf_op jit(solution)/shard_map/reshape | solution.py:91
  3.2 0.1 copy.9
  3.4 0.1 pad_maximum_fusion
  3.5 36.7 %all_to_all.15 = bf16[32,112,128]{2,1,0:T(8,128)(2,1)S(1)} all-to-all(bf16[32,112,128]{2,1,0:T(8,128)(2,1)S(1)} %pad_maximum_fusion), channel_id=1, replica_groups=mesh['doc'=8,'seq'=32] {'seq'}, dimensions={0} | all-to-all | bytes 1835008 | tf_op jit(solution)/shard_map/all_to_all | solution.py:96
  40.2 0.1 fusion
  40.2 0.1 reshape.82
  40.3 0.0 copy-done.1
  40.4 0.1 select_reduce_fusion
  40.4 0.1 reshape.77
  40.5 0.1 reshape.93
  40.7 0.1 slice.43
  40.7 2.6 %gather_fusion.1 = bf16[128,96,128]{2,1,0:T(8,128)(2,1)} fusion(bf16[32,96,128]{2,1,0:T(8,128)(2,1)S(1)} %slice.43, s32[1024]{0:T(1024)S(1)} %pad_clamp_fusion), kind=kCustom, calls=%fused_computation.1 | custom fusion | bytes 6291968 | tf_op jit(solution)/shard_map/jit(_take)/gather | solution.py:102
  43.4 5.3 %all-to-all-start.2 = ((bf16[32,4,96,128]{3,2,1,0:T(8,128)(2,1)}), bf16[32,4,96,128]{3,2,1,0:T(8,128)(2,1)}, u32[]{:S(2)}, u32[]{:S(2)}) async-start(bf16[32,4,96,128]{3,2,1,0:T(8,128)(2,1)} %bitcast.11), calls=%async_computation.2 | async-start | bytes 6291456 | tf_op jit(solution)/shard_map/all_to_all | solution.py:106
  48.7 0.2 slice_reduce_fusion
  48.9 1.5 gather_fusion
  50.4 69.3 %all-to-all-done.2 = bf16[32,4,96,128]{3,2,1,0:T(8,128)(2,1)} async-done(((bf16[32,4,96,128]{3,2,1,0:T(8,128)(2,1)}), bf16[32,4,96,128]{3,2,1,0:T(8,128)(2,1)}, u32[]{:S(2)}, u32[]{:S(2)}) %all-to-all-start.2) | async-done | bytes 3145760 | tf_op jit(solution)/shard_map/all_to_all | solution.py:106
  119.8 6.3 %all-to-all-start.1 = ((bf16[32,1,96,128]{3,2,1,0:T(8,128)(2,1)}), bf16[32,1,96,128]{3,2,1,0:T(8,128)(2,1)S(1)}, u32[]{:S(2)}, u32[]{:S(2)}) async-start(bf16[32,1,96,128]{3,2,1,0:T(8,128)(2,1)} %bitcast.4), calls=%async_computation.1 | async-start | bytes 1572864 | tf_op jit(solution)/shard_map/all_to_all | solution.py:107
  126.1 15.2 %shard_map.46.refs_0_ = bf16[640,4096]{1,0:T(8,128)(2,1)} custom-call(s32[5]{0:T(128)} %image_ref.3, bf16[640,4096]{1,0:T(8,128)(2,1)} %q_ref.3, bf16[4,2,4,4,96,128]{5,4,3,2,1,0:T(8,128)(2,1)} %bitcast.7.kv_ref), custom_call_target="tpu_custom_call" | custom-call | tf_op jit(solution)/shard_map/pallas_call | solution.py:70
  141.2 6.1 %all-to-all-done.1 = bf16[32,1,96,128]{3,2,1,0:T(8,128)(2,1)S(1)} async-done(((bf16[32,1,96,128]{3,2,1,0:T(8,128)(2,1)}), bf16[32,1,96,128]{3,2,1,0:T(8,128)(2,1)S(1)}, u32[]{:S(2)}, u32[]{:S(2)}) %all-to-all-start.1) | async-done | bytes 786464 | tf_op jit(solution)/shard_map/all_to_all | solution.py:107
  147.3 0.0 copy-start
  147.3 0.9 copy-done
  148.2 6.2 %shard_map.47 = bf16[640,4096]{1,0:T(8,128)(2,1)} custom-call(s32[5]{0:T(128)} %image_ref.3, bf16[640,4096]{1,0:T(8,128)(2,1)} %q_ref.3, bf16[4,2,4,1,96,128]{5,4,3,2,1,0:T(8,128)(2,1)} %bitcast.12, bf16[640,4096]{1,0:T(8,128)(2,1)} %shard_map.46.refs_0_), custom_call_target="tpu_custom_call", output_to_operand_aliasing={{}: (3, {})} | custom-call | tf_op jit(solution)/shard_map/pallas_call | solution.py:70
  (4 shorter events, 0.0 us)
Async XLA Ops:
  0.7 39.7 %copy-start.1 = (s32[32]{0:T(128)S(1)}, s32[32]{0:T(128)}, u32[]{:S(2)}) copy-start(s32[32]{0:T(128)} %param.9) | copy-start | bytes 388
  43.4 76.4 %all-to-all-start.2 = ((bf16[32,4,96,128]{3,2,1,0:T(8,128)(2,1)}), bf16[32,4,96,128]{3,2,1,0:T(8,128)(2,1)}, u32[]{:S(2)}, u32[]{:S(2)}) async-start(bf16[32,4,96,128]{3,2,1,0:T(8,128)(2,1)} %bitcast.11), calls=%async_computation.2 | async-start | bytes 6291456 | tf_op jit(solution)/shard_map/all_to_all | solution.py:106
  119.8 27.6 %all-to-all-start.1 = ((bf16[32,1,96,128]{3,2,1,0:T(8,128)(2,1)}), bf16[32,1,96,128]{3,2,1,0:T(8,128)(2,1)S(1)}, u32[]{:S(2)}, u32[]{:S(2)}) async-start(bf16[32,1,96,128]{3,2,1,0:T(8,128)(2,1)} %bitcast.4), calls=%async_computation.1 | async-start | bytes 1572864 | tf_op jit(solution)/shard_map/all_to_all | solution.py:107
  147.3 0.9 copy-start

commit v9 on v7

--- a/solution.py
+++ b/solution.py
@@ -74,6 +74,33 @@
     )(*operands)
 
 
+def attend_late(queries, kv_shares, block_image, first, previous):
+    row_count, row_width = queries.shape
+    kv_local, _, row_groups, count_blocks, share_rows, _ = kv_shares.shape
+    group_size = row_width // (HD * kv_local)
+    q_late = lax.slice_in_dim(queries, first * BLOCK, (first + count_blocks) * BLOCK, axis=0)
+    kernel = functools.partial(
+        attend_kernel, group_size=group_size, kv_local=kv_local,
+        memory_rows=row_groups * share_rows, first=first,
+    )
+    grid_spec = pltpu.PrefetchScalarGridSpec(
+        num_scalar_prefetch=1,
+        grid=(count_blocks,),
+        in_specs=[
+            pl.BlockSpec(memory_space=pltpu.VMEM),
+            pl.BlockSpec(memory_space=pltpu.VMEM),
+            pl.BlockSpec(memory_space=pl.ANY),
+        ],
+        out_specs=pl.BlockSpec((BLOCK, row_width), lambda b, img: (b + first, 0)),
+    )
+    return pl.pallas_call(
+        kernel,
+        grid_spec=grid_spec,
+        out_shape=jax.ShapeDtypeStruct(queries.shape, queries.dtype),
+        input_output_aliases={3: 0},
+    )(block_image, q_late, kv_shares.reshape(kv_local, 2, row_groups * count_blocks, share_rows, HD), previous)
+
+
 def holder_of(image_ids, image_slot):
     image_count = image_slot.shape[0]
     same_image = image_ids[:, None] == jnp.arange(image_count, dtype=jnp.int32)[None, :]
@@ -107,7 +134,7 @@
     early = early.reshape(kv_local, 2, row_groups, split, share_rows, HD)
     late = late.reshape(kv_local, 2, row_groups, own_blocks - split, share_rows, HD)
     result = attend(queries, early, block_image, 0)
-    return attend(queries, late, block_image, split, result)
+    return attend_late(queries, late, block_image, split, result)
 
 
 def solution(mesh):

time: 155 us -> 155 us (level)
  local copies, waits for them, and re-layouts: 8.28 us -> 10.6 us
  waiting for transfers between devices: 75.4 us -> 73.1 us
    pallas_call x2 -> x1, Pallas kernels: 21.2 us -> 15.2 us  [attend(): pl.pallas_call(kernel, grid_spec=grid_spec, out_shape=jax.ShapeDtypeStruc...]
    pallas_call x0 -> x1, Pallas kernels: none -> 6.07 us  [attend_late(): pl.pallas_call(kernel, grid_spec=grid_spec, out_shape=jax.ShapeDtypeStruc...]
    slice x0 -> x1, local copies, waits for them, and re-layouts: none -> 2.3 us  [attend_late(): lax.slice_in_dim(queries, first * BLOCK, (first + count_blocks) * BLOCK,...]
    all_to_all x1, waiting for transfers between devices: 6.12 us -> 3.82 us  [local(): late = lax.all_to_all(late, 'seq', split_axis=0, concat_axis=0, tiled=True)]
  transfers between devices with their start and end apart: 2 -> 2, of which waited for: 2 -> 2; matrix products, arithmetic and copies ran while one was open for 1% -> 3% of each run, Pallas kernels for 10% -> 10%
where the time goes in v9:
time: 155 us; the launch traced here: 154 us
  waiting for transfers between devices  73.1 us (47%)
  blocking collectives  36.7 us (24%)
  Pallas kernels  21.2 us (14%)
  starting transfers between devices  11.6 us (7%)
  local copies, waits for them, and re-layouts  10.6 us (7%)
    all_to_all x1, waiting for transfers between devices, local(): lax.all_to_all(early, 'seq', split_axis=0, concat_axis=0, tiled=True)  69.3 us
    all_to_all x1, blocking collectives, local(): lax.all_to_all(payload, 'seq', split_axis=0, concat_axis=0, tiled=True)  36.7 us
    pallas_call x1, Pallas kernels, attend(): pl.pallas_call(kernel, grid_spec=grid_spec, out_shape=jax.ShapeDtypeStruc...  15.2 us
    all_to_all x1, starting transfers between devices, local(): late = lax.all_to_all(late, 'seq', split_axis=0, concat_axis=0, tiled=True)  6.29 us
    pallas_call x1, Pallas kernels, attend_late(): pl.pallas_call(kernel, grid_spec=grid_spec, out_shape=jax.ShapeDtypeStruc...  6.07 us
    all_to_all x1, starting transfers between devices, local(): lax.all_to_all(early, 'seq', split_axis=0, concat_axis=0, tiled=True)  5.34 us
    all_to_all x1, waiting for transfers between devices, local(): late = lax.all_to_all(late, 'seq', split_axis=0, concat_axis=0, tiled=True)  3.82 us
  transfers between devices with their start and end apart: 2, of which 2 were waited for; matrix products, arithmetic and copies ran while one was open for 3% of the time, Pallas kernels for 10%

profile of v9, /device:TPU:16, one launch (start us, length us, event | category | flops | bytes accessed | tf_op | source)
XLA Modules:
  0.0 154.3 jit_solution(12292554006820030583)
XLA Ops:
  0.0 0.7 convert_bitcast_fusion
  0.7 0.0 copy-start.1
  0.7 2.6 %reshape.71 = bf16[4,96,4,2,128]{4,3,2,1,0:T(2,128)(2,1)S(1)} reshape(bf16[1,384,1024]{2,1,0:T(8,128)(2,1)} %param.7) | data formatting | bytes 1572864 | tf_op jit(solution)/shard_map/reshape | solution.py:117
  3.2 0.1 copy.9
  3.4 0.1 pad_maximum_fusion
  3.5 36.7 %all_to_all.15 = bf16[32,112,128]{2,1,0:T(8,128)(2,1)S(1)} all-to-all(bf16[32,112,128]{2,1,0:T(8,128)(2,1)S(1)} %pad_maximum_fusion), channel_id=1, replica_groups=mesh['doc'=8,'seq'=32] {'seq'}, dimensions={0} | all-to-all | bytes 1835008 | tf_op jit(solution)/shard_map/all_to_all | solution.py:122
  40.2 0.1 fusion
  40.2 0.1 reshape.78
  40.3 0.0 copy-done.1
  40.4 0.1 select_reduce_fusion
  40.4 0.1 reshape.74
  40.5 0.1 reshape.89
  40.7 0.1 slice.47
  40.7 2.6 %gather_fusion.1 = bf16[128,96,128]{2,1,0:T(8,128)(2,1)} fusion(bf16[32,96,128]{2,1,0:T(8,128)(2,1)S(1)} %slice.47, s32[1024]{0:T(1024)S(1)} %pad_clamp_fusion), kind=kCustom, calls=%fused_computation.1 | custom fusion | bytes 6291968 | tf_op jit(solution)/shard_map/jit(_take)/gather | solution.py:128
  43.4 5.3 %all-to-all-start.2 = ((bf16[32,4,96,128]{3,2,1,0:T(8,128)(2,1)}), bf16[32,4,96,128]{3,2,1,0:T(8,128)(2,1)}, u32[]{:S(2)}, u32[]{:S(2)}) async-start(bf16[32,4,96,128]{3,2,1,0:T(8,128)(2,1)} %bitcast.11), calls=%async_computation.2 | async-start | bytes 6291456 | tf_op jit(solution)/shard_map/all_to_all | solution.py:132
  48.7 0.2 slice_reduce_fusion
  48.9 1.5 gather_fusion
  50.4 69.3 %all-to-all-done.2 = bf16[32,4,96,128]{3,2,1,0:T(8,128)(2,1)} async-done(((bf16[32,4,96,128]{3,2,1,0:T(8,128)(2,1)}), bf16[32,4,96,128]{3,2,1,0:T(8,128)(2,1)}, u32[]{:S(2)}, u32[]{:S(2)}) %all-to-all-start.2) | async-done | bytes 3145760 | tf_op jit(solution)/shard_map/all_to_all | solution.py:132
  119.8 6.3 %all-to-all-start.1 = ((bf16[32,1,96,128]{3,2,1,0:T(8,128)(2,1)}), bf16[32,1,96,128]{3,2,1,0:T(8,128)(2,1)S(1)}, u32[]{:S(2)}, u32[]{:S(2)}) async-start(bf16[32,1,96,128]{3,2,1,0:T(8,128)(2,1)} %bitcast.4), calls=%async_computation.1 | async-start | bytes 1572864 | tf_op jit(solution)/shard_map/all_to_all | solution.py:133
  126.1 2.3 %slice.38.q_ref = bf16[128,4096]{1,0:T(8,128)(2,1)} slice(bf16[640,4096]{1,0:T(8,128)(2,1)} %q_ref.1), slice={[512:640], [0:4096]} | slice | bytes 2097152 | tf_op jit(solution)/shard_map/slice | solution.py:81
  128.4 15.2 %shard_map.46.refs_0_ = bf16[640,4096]{1,0:T(8,128)(2,1)} custom-call(s32[5]{0:T(128)} %image_ref.3, bf16[640,4096]{1,0:T(8,128)(2,1)} %q_ref.1, bf16[4,2,4,4,96,128]{5,4,3,2,1,0:T(8,128)(2,1)} %bitcast.7.kv_ref), custom_call_target="tpu_custom_call" | custom-call | tf_op jit(solution)/shard_map/pallas_call | solution.py:69
  143.5 3.8 %all-to-all-done.1 = bf16[32,1,96,128]{3,2,1,0:T(8,128)(2,1)S(1)} async-done(((bf16[32,1,96,128]{3,2,1,0:T(8,128)(2,1)}), bf16[32,1,96,128]{3,2,1,0:T(8,128)(2,1)S(1)}, u32[]{:S(2)}, u32[]{:S(2)}) %all-to-all-start.1) | async-done | bytes 786464 | tf_op jit(solution)/shard_map/all_to_all | solution.py:133
  147.3 0.9 copy-done
  148.2 6.1 %shard_map.47 = bf16[640,4096]{1,0:T(8,128)(2,1)} custom-call(s32[5]{0:T(128)} %image_ref.3, bf16[128,4096]{1,0:T(8,128)(2,1)} %slice.38.q_ref, bf16[4,2,4,96,128]{4,3,2,1,0:T(8,128)(2,1)} %bitcast.12, bf16[640,4096]{1,0:T(8,128)(2,1)} %shard_map.46.refs_0_), custom_call_target="tpu_custom_call", output_to_operand_aliasing={{}: (3, {})} | custom-call | tf_op jit(solution)/shard_map/pallas_call | solution.py:96
  (5 shorter events, 0.0 us)
Async XLA Ops:
  0.7 39.7 %copy-start.1 = (s32[32]{0:T(128)S(1)}, s32[32]{0:T(128)}, u32[]{:S(2)}) copy-start(s32[32]{0:T(128)} %param.9) | copy-start | bytes 388
  43.4 76.4 %all-to-all-start.2 = ((bf16[32,4,96,128]{3,2,1,0:T(8,128)(2,1)}), bf16[32,4,96,128]{3,2,1,0:T(8,128)(2,1)}, u32[]{:S(2)}, u32[]{:S(2)}) async-start(bf16[32,4,96,128]{3,2,1,0:T(8,128)(2,1)} %bitcast.11), calls=%async_computation.2 | async-start | bytes 6291456 | tf_op jit(solution)/shard_map/all_to_all | solution.py:132
  119.8 27.6 %all-to-all-start.1 = ((bf16[32,1,96,128]{3,2,1,0:T(8,128)(2,1)}), bf16[32,1,96,128]{3,2,1,0:T(8,128)(2,1)S(1)}, u32[]{:S(2)}, u32[]{:S(2)}) async-start(bf16[32,1,96,128]{3,2,1,0:T(8,128)(2,1)} %bitcast.4), calls=%async_computation.1 | async-start | bytes 1572864 | tf_op jit(solution)/shard_map/all_to_all | solution.py:133
  147.3 0.9 copy-start

commit v10 on v9

--- a/solution.py
+++ b/solution.py
@@ -101,6 +101,41 @@
     )(block_image, q_late, kv_shares.reshape(kv_local, 2, row_groups * count_blocks, share_rows, HD), previous)
 
 
+def pack_kernel(image_ref, kv_ref, out_ref, *, row_groups, share_rows, parts, own_blocks):
+    row = lax.broadcasted_iota(jnp.int32, (TAG_ROWS, HD), 0)
+    lane = lax.broadcasted_iota(jnp.int32, (TAG_ROWS, HD), 1)
+    tag = jnp.zeros((TAG_ROWS, HD), jnp.float32)
+    for i in range(own_blocks):
+        tag = jnp.where((row == 0) & (lane == i), image_ref[i].astype(jnp.float32), tag)
+    tag = tag.astype(out_ref.dtype)
+    for part in range(parts):
+        for rg in range(row_groups):
+            c = part * row_groups + rg
+            out_ref[c, :share_rows, :] = kv_ref[rg * share_rows:(rg + 1) * share_rows, part * HD:(part + 1) * HD]
+            out_ref[c, share_rows:, :] = tag
+
+
+def pack_shares(memory_kv, block_image, row_groups, share_rows):
+    _, img_rows, kv_width = memory_kv.shape
+    parts = kv_width // HD
+    count = parts * row_groups
+    kernel = functools.partial(
+        pack_kernel, row_groups=row_groups, share_rows=share_rows, parts=parts,
+        own_blocks=block_image.shape[0],
+    )
+    grid_spec = pltpu.PrefetchScalarGridSpec(
+        num_scalar_prefetch=1,
+        grid=(1,),
+        in_specs=[pl.BlockSpec((None, img_rows, kv_width), lambda i, img: (0, 0, 0))],
+        out_specs=pl.BlockSpec((count, share_rows + TAG_ROWS, HD), lambda i, img: (0, 0, 0)),
+    )
+    return pl.pallas_call(
+        kernel,
+        grid_spec=grid_spec,
+        out_shape=jax.ShapeDtypeStruct((count, share_rows + TAG_ROWS, HD), memory_kv.dtype),
+    )(block_image, memory_kv)
+
+
 def holder_of(image_ids, image_slot):
     image_count = image_slot.shape[0]
     same_image = image_ids[:, None] == jnp.arange(image_count, dtype=jnp.int32)[None, :]
@@ -114,11 +149,7 @@
     kv_local = kv_width // (2 * HD)
     row_groups = seq_count // (2 * kv_local)
     share_rows = img_rows // row_groups
-    shares = memory_kv.reshape(row_groups, share_rows, kv_local, 2, HD)
-    shares = shares.transpose(2, 3, 0, 1, 4).reshape(seq_count, share_rows, HD)
-    tag = jnp.zeros((seq_count, TAG_ROWS, HD), shares.dtype)
-    tag = tag.at[:, 0, :own_blocks].set(block_image.astype(shares.dtype)[None, :])
-    payload = jnp.concatenate([shares, tag], axis=1)
+    payload = pack_shares(memory_kv, block_image, row_groups, share_rows)
     held = lax.all_to_all(payload, "seq", split_axis=0, concat_axis=0, tiled=True)
     wanted = held[:, share_rows, :own_blocks].astype(jnp.int32).reshape(seq_count * own_blocks)
     wanted_slot = holder_of(wanted, image_slot)

time: 155 us -> 154 us (level)
  Pallas kernels: 21.2 us -> 24.2 us
  local copies, waits for them, and re-layouts: 10.6 us -> 7.87 us
    pallas_call x0 -> x1, Pallas kernels: none -> 2.99 us  [pack_shares(): pl.pallas_call(kernel, grid_spec=grid_spec, out_shape=jax.ShapeDtypeStruc...]
    reshape x1 -> x0, local copies, waits for them, and re-layouts: 2.57 us -> none  [local(): shares = memory_kv.reshape(row_groups, share_rows, kv_local, 2, HD)]
where the time goes in v10:
time: 154 us
  waiting for transfers between devices  73.1 us (47%)
  blocking collectives  36.9 us (24%)
  Pallas kernels  24.2 us (16%)
  starting transfers between devices  11.6 us (8%)
  local copies, waits for them, and re-layouts  7.87 us (5%)
    all_to_all x1, waiting for transfers between devices, local(): lax.all_to_all(early, 'seq', split_axis=0, concat_axis=0, tiled=True)  69.3 us
    all_to_all x1, blocking collectives, local(): lax.all_to_all(payload, 'seq', split_axis=0, concat_axis=0, tiled=True)  36.9 us
    pallas_call x1, Pallas kernels, attend(): pl.pallas_call(kernel, grid_spec=grid_spec, out_shape=jax.ShapeDtypeStruc...  15.2 us
    all_to_all x1, starting transfers between devices, local(): late = lax.all_to_all(late, 'seq', split_axis=0, concat_axis=0, tiled=True)  6.29 us
    pallas_call x1, Pallas kernels, attend_late(): pl.pallas_call(kernel, grid_spec=grid_spec, out_shape=jax.ShapeDtypeStruc...  6.07 us
    all_to_all x1, starting transfers between devices, local(): lax.all_to_all(early, 'seq', split_axis=0, concat_axis=0, tiled=True)  5.34 us
    all_to_all x1, waiting for transfers between devices, local(): late = lax.all_to_all(late, 'seq', split_axis=0, concat_axis=0, tiled=True)  3.82 us
  transfers between devices with their start and end apart: 2, of which 2 were waited for; matrix products, arithmetic and copies ran while one was open for 3% of the time, Pallas kernels for 10%

profile of v10, /device:TPU:16, one launch (start us, length us, event | category | flops | bytes accessed | tf_op | source)
XLA Modules:
  0.0 154.0 jit_solution(15816160407764867859)
XLA Ops:
  0.0 0.0 copy-start.1
  0.0 3.0 %shard_map.46 = bf16[32,112,128]{2,1,0:T(8,128)(2,1)} custom-call(s32[5]{0:T(128)} %image_ref.5, bf16[1,384,1024]{2,1,0:T(8,128)(2,1)} %kv_ref.1), custom_call_target="tpu_custom_call" | custom-call | tf_op jit(solution)/shard_map/pallas_call | solution.py:132
  3.0 36.9 %all_to_all.15 = bf16[32,112,128]{2,1,0:T(8,128)(2,1)S(1)} all-to-all(bf16[32,112,128]{2,1,0:T(8,128)(2,1)} %shard_map.46), channel_id=1, replica_groups=mesh['doc'=8,'seq'=32] {'seq'}, dimensions={0} | all-to-all | bytes 1835008 | tf_op jit(solution)/shard_map/all_to_all | solution.py:153
  39.9 0.1 fusion
  40.0 0.1 reshape.27
  40.1 0.0 copy-done.1
  40.1 0.1 select_reduce_fusion
  40.2 0.1 reshape.23
  40.3 0.1 reshape.38
  40.4 0.1 slice.24
  40.5 2.6 %gather_fusion.1 = bf16[128,96,128]{2,1,0:T(8,128)(2,1)} fusion(bf16[32,96,128]{2,1,0:T(8,128)(2,1)S(1)} %slice.24, s32[1024]{0:T(1024)S(1)} %pad_clamp_fusion), kind=kCustom, calls=%fused_computation.1 | custom fusion | bytes 6291968 | tf_op jit(solution)/shard_map/jit(_take)/gather | solution.py:159
  43.1 5.3 %all-to-all-start.2 = ((bf16[32,4,96,128]{3,2,1,0:T(8,128)(2,1)}), bf16[32,4,96,128]{3,2,1,0:T(8,128)(2,1)}, u32[]{:S(2)}, u32[]{:S(2)}) async-start(bf16[32,4,96,128]{3,2,1,0:T(8,128)(2,1)} %bitcast.7), calls=%async_computation.2 | async-start | bytes 6291456 | tf_op jit(solution)/shard_map/all_to_all | solution.py:163
  48.4 0.2 slice_reduce_fusion
  48.6 1.5 gather_fusion
  50.1 69.3 %all-to-all-done.2 = bf16[32,4,96,128]{3,2,1,0:T(8,128)(2,1)} async-done(((bf16[32,4,96,128]{3,2,1,0:T(8,128)(2,1)}), bf16[32,4,96,128]{3,2,1,0:T(8,128)(2,1)}, u32[]{:S(2)}, u32[]{:S(2)}) %all-to-all-start.2) | async-done | bytes 3145760 | tf_op jit(solution)/shard_map/all_to_all | solution.py:163
  119.5 6.3 %all-to-all-start.1 = ((bf16[32,1,96,128]{3,2,1,0:T(8,128)(2,1)}), bf16[32,1,96,128]{3,2,1,0:T(8,128)(2,1)S(1)}, u32[]{:S(2)}, u32[]{:S(2)}) async-start(bf16[32,1,96,128]{3,2,1,0:T(8,128)(2,1)} %bitcast.1), calls=%async_computation.1 | async-start | bytes 1572864 | tf_op jit(solution)/shard_map/all_to_all | solution.py:164
  125.8 2.3 %slice.15.q_ref = bf16[128,4096]{1,0:T(8,128)(2,1)} slice(bf16[640,4096]{1,0:T(8,128)(2,1)} %q_ref.1), slice={[512:640], [0:4096]} | slice | bytes 2097152 | tf_op jit(solution)/shard_map/slice | solution.py:81
  128.1 15.2 %shard_map.47.refs_0_ = bf16[640,4096]{1,0:T(8,128)(2,1)} custom-call(s32[5]{0:T(128)} %image_ref.5, bf16[640,4096]{1,0:T(8,128)(2,1)} %q_ref.1, bf16[4,2,4,4,96,128]{5,4,3,2,1,0:T(8,128)(2,1)} %bitcast.4.kv_ref), custom_call_target="tpu_custom_call" | custom-call | tf_op jit(solution)/shard_map/pallas_call | solution.py:69
  143.2 3.8 %all-to-all-done.1 = bf16[32,1,96,128]{3,2,1,0:T(8,128)(2,1)S(1)} async-done(((bf16[32,1,96,128]{3,2,1,0:T(8,128)(2,1)}), bf16[32,1,96,128]{3,2,1,0:T(8,128)(2,1)S(1)}, u32[]{:S(2)}, u32[]{:S(2)}) %all-to-all-start.1) | async-done | bytes 786464 | tf_op jit(solution)/shard_map/all_to_all | solution.py:164
  147.0 0.0 copy-start
  147.0 0.9 copy-done
  147.9 6.1 %shard_map.48 = bf16[640,4096]{1,0:T(8,128)(2,1)} custom-call(s32[5]{0:T(128)} %image_ref.5, bf16[128,4096]{1,0:T(8,128)(2,1)} %slice.15.q_ref, bf16[4,2,4,96,128]{4,3,2,1,0:T(8,128)(2,1)} %bitcast.8, bf16[640,4096]{1,0:T(8,128)(2,1)} %shard_map.47.refs_0_), custom_call_target="tpu_custom_call", output_to_operand_aliasing={{}: (3, {})} | custom-call | tf_op jit(solution)/shard_map/pallas_call | solution.py:96
  (2 shorter events, 0.0 us)
Async XLA Ops:
  0.0 40.1 %copy-start.1 = (s32[32]{0:T(128)S(1)}, s32[32]{0:T(128)}, u32[]{:S(2)}) copy-start(s32[32]{0:T(128)} %param.7) | copy-start | bytes 388
  43.1 76.4 %all-to-all-start.2 = ((bf16[32,4,96,128]{3,2,1,0:T(8,128)(2,1)}), bf16[32,4,96,128]{3,2,1,0:T(8,128)(2,1)}, u32[]{:S(2)}, u32[]{:S(2)}) async-start(bf16[32,4,96,128]{3,2,1,0:T(8,128)(2,1)} %bitcast.7), calls=%async_computation.2 | async-start | bytes 6291456 | tf_op jit(solution)/shard_map/all_to_all | solution.py:163
  119.5 27.6 %all-to-all-start.1 = ((bf16[32,1,96,128]{3,2,1,0:T(8,128)(2,1)}), bf16[32,1,96,128]{3,2,1,0:T(8,128)(2,1)S(1)}, u32[]{:S(2)}, u32[]{:S(2)}) async-start(bf16[32,1,96,128]{3,2,1,0:T(8,128)(2,1)} %bitcast.1), calls=%async_computation.1 | async-start | bytes 1572864 | tf_op jit(solution)/shard_map/all_to_all | solution.py:164
  147.0 0.9 copy-start

commit v11 on v8

--- a/solution.py
+++ b/solution.py
@@ -108,7 +108,7 @@
     early = early.reshape(kv_local, 2, row_groups, split, share_rows, HD)
     late = late.reshape(kv_local, 2, row_groups, own_blocks - split, share_rows, HD)
     result = attend(queries, early, block_image, 0, kv_local)
-    return attend(queries, late, block_image, split, 1, result)
+    return attend(queries, late, block_image, split, kv_local // 2, result)
 
 
 def solution(mesh):

time: 155 us -> 154 us (level)
  no operation moved by 1% of the time
where the time goes in v11:
time: 154 us
  waiting for transfers between devices  75.4 us (49%)
  blocking collectives  36.7 us (24%)
  Pallas kernels  21 us (14%)
  starting transfers between devices  11.6 us (8%)
  local copies, waits for them, and re-layouts  8.28 us (5%)
    all_to_all x1, waiting for transfers between devices, local(): lax.all_to_all(early, 'seq', split_axis=0, concat_axis=0, tiled=True)  69.3 us
    all_to_all x1, blocking collectives, local(): lax.all_to_all(payload, 'seq', split_axis=0, concat_axis=0, tiled=True)  36.7 us
    pallas_call x2, Pallas kernels, attend(): pl.pallas_call(kernel, grid_spec=grid_spec, out_shape=jax.ShapeDtypeStruc...  21 us
    all_to_all x1, starting transfers between devices, local(): late = lax.all_to_all(late, 'seq', split_axis=0, concat_axis=0, tiled=True)  6.29 us
    all_to_all x1, waiting for transfers between devices, local(): late = lax.all_to_all(late, 'seq', split_axis=0, concat_axis=0, tiled=True)  6.12 us
    all_to_all x1, starting transfers between devices, local(): lax.all_to_all(early, 'seq', split_axis=0, concat_axis=0, tiled=True)  5.34 us
  transfers between devices with their start and end apart: 2, of which 2 were waited for; matrix products, arithmetic and copies ran while one was open for 1% of the time, Pallas kernels for 10%

profile of v11, /device:TPU:16, one launch (start us, length us, event | category | flops | bytes accessed | tf_op | source)
XLA Modules:
  0.0 154.0 jit_solution(11630643380051182997)
XLA Ops:
  0.0 0.7 convert_bitcast_fusion
  0.7 0.0 copy-start.1
  0.7 2.6 %reshape.74 = bf16[4,96,4,2,128]{4,3,2,1,0:T(2,128)(2,1)S(1)} reshape(bf16[1,384,1024]{2,1,0:T(8,128)(2,1)} %param.7) | data formatting | bytes 1572864 | tf_op jit(solution)/shard_map/reshape | solution.py:91
  3.2 0.1 copy.9
  3.4 0.1 pad_maximum_fusion
  3.5 36.7 %all_to_all.15 = bf16[32,112,128]{2,1,0:T(8,128)(2,1)S(1)} all-to-all(bf16[32,112,128]{2,1,0:T(8,128)(2,1)S(1)} %pad_maximum_fusion), channel_id=1, replica_groups=mesh['doc'=8,'seq'=32] {'seq'}, dimensions={0} | all-to-all | bytes 1835008 | tf_op jit(solution)/shard_map/all_to_all | solution.py:96
  40.2 0.1 fusion
  40.2 0.1 reshape.82
  40.3 0.0 copy-done.1
  40.4 0.1 select_reduce_fusion
  40.4 0.1 reshape.77
  40.5 0.1 reshape.93
  40.7 0.1 slice.43
  40.7 2.6 %gather_fusion.1 = bf16[128,96,128]{2,1,0:T(8,128)(2,1)} fusion(bf16[32,96,128]{2,1,0:T(8,128)(2,1)S(1)} %slice.43, s32[1024]{0:T(1024)S(1)} %pad_clamp_fusion), kind=kCustom, calls=%fused_computation.1 | custom fusion | bytes 6291968 | tf_op jit(solution)/shard_map/jit(_take)/gather | solution.py:102
  43.4 5.3 %all-to-all-start.2 = ((bf16[32,4,96,128]{3,2,1,0:T(8,128)(2,1)}), bf16[32,4,96,128]{3,2,1,0:T(8,128)(2,1)}, u32[]{:S(2)}, u32[]{:S(2)}) async-start(bf16[32,4,96,128]{3,2,1,0:T(8,128)(2,1)} %bitcast.11), calls=%async_computation.2 | async-start | bytes 6291456 | tf_op jit(solution)/shard_map/all_to_all | solution.py:106
  48.7 0.2 slice_reduce_fusion
  48.9 1.5 gather_fusion
  50.4 69.3 %all-to-all-done.2 = bf16[32,4,96,128]{3,2,1,0:T(8,128)(2,1)} async-done(((bf16[32,4,96,128]{3,2,1,0:T(8,128)(2,1)}), bf16[32,4,96,128]{3,2,1,0:T(8,128)(2,1)}, u32[]{:S(2)}, u32[]{:S(2)}) %all-to-all-start.2) | async-done | bytes 3145760 | tf_op jit(solution)/shard_map/all_to_all | solution.py:106
  119.8 6.3 %all-to-all-start.1 = ((bf16[32,1,96,128]{3,2,1,0:T(8,128)(2,1)}), bf16[32,1,96,128]{3,2,1,0:T(8,128)(2,1)S(1)}, u32[]{:S(2)}, u32[]{:S(2)}) async-start(bf16[32,1,96,128]{3,2,1,0:T(8,128)(2,1)} %bitcast.4), calls=%async_computation.1 | async-start | bytes 1572864 | tf_op jit(solution)/shard_map/all_to_all | solution.py:107
  126.1 15.2 %shard_map.46.refs_0_ = bf16[640,4096]{1,0:T(8,128)(2,1)} custom-call(s32[5]{0:T(128)} %image_ref.3, bf16[640,4096]{1,0:T(8,128)(2,1)} %q_ref.3, bf16[4,2,4,4,96,128]{5,4,3,2,1,0:T(8,128)(2,1)} %bitcast.7.kv_ref), custom_call_target="tpu_custom_call" | custom-call | tf_op jit(solution)/shard_map/pallas_call | solution.py:70
  141.2 6.1 %all-to-all-done.1 = bf16[32,1,96,128]{3,2,1,0:T(8,128)(2,1)S(1)} async-done(((bf16[32,1,96,128]{3,2,1,0:T(8,128)(2,1)}), bf16[32,1,96,128]{3,2,1,0:T(8,128)(2,1)S(1)}, u32[]{:S(2)}, u32[]{:S(2)}) %all-to-all-start.1) | async-done | bytes 786464 | tf_op jit(solution)/shard_map/all_to_all | solution.py:107
  147.3 0.0 copy-start
  147.3 0.9 copy-done
  148.2 5.8 %shard_map.47 = bf16[640,4096]{1,0:T(8,128)(2,1)} custom-call(s32[5]{0:T(128)} %image_ref.3, bf16[640,4096]{1,0:T(8,128)(2,1)} %q_ref.3, bf16[4,2,4,1,96,128]{5,4,3,2,1,0:T(8,128)(2,1)} %bitcast.12, bf16[640,4096]{1,0:T(8,128)(2,1)} %shard_map.46.refs_0_), custom_call_target="tpu_custom_call", output_to_operand_aliasing={{}: (3, {})} | custom-call | tf_op jit(solution)/shard_map/pallas_call | solution.py:70
  (4 shorter events, 0.0 us)
Async XLA Ops:
  0.7 39.7 %copy-start.1 = (s32[32]{0:T(128)S(1)}, s32[32]{0:T(128)}, u32[]{:S(2)}) copy-start(s32[32]{0:T(128)} %param.9) | copy-start | bytes 388
  43.4 76.4 %all-to-all-start.2 = ((bf16[32,4,96,128]{3,2,1,0:T(8,128)(2,1)}), bf16[32,4,96,128]{3,2,1,0:T(8,128)(2,1)}, u32[]{:S(2)}, u32[]{:S(2)}) async-start(bf16[32,4,96,128]{3,2,1,0:T(8,128)(2,1)} %bitcast.11), calls=%async_computation.2 | async-start | bytes 6291456 | tf_op jit(solution)/shard_map/all_to_all | solution.py:106
  119.8 27.6 %all-to-all-start.1 = ((bf16[32,1,96,128]{3,2,1,0:T(8,128)(2,1)}), bf16[32,1,96,128]{3,2,1,0:T(8,128)(2,1)S(1)}, u32[]{:S(2)}, u32[]{:S(2)}) async-start(bf16[32,1,96,128]{3,2,1,0:T(8,128)(2,1)} %bitcast.4), calls=%async_computation.1 | async-start | bytes 1572864 | tf_op jit(solution)/shard_map/all_to_all | solution.py:107
  147.3 0.9 copy-start
